TPU v7x, 128 devices: a whole 4x4x4 slice. The times are simulated.
128 devices in a mesh: ctx: 16 (over x, y_hi, core), head: 8 (over z, y_lo).
Axes of the slice: x: 4, y: 4 (y_hi: 2, y_lo: 2; y = y_hi * 2 + y_lo), z: 4, core: 2. Of those that a mesh axis runs over, the one named last changes fastest.
Arguments:
- activations: bfloat16 [8192, 4096], P('ctx')
- qkv_weight: bfloat16 [4096, 3, 32, 128], P(None, None, 'head'), may hold values from -0.09375 to 0.09375
- out_weight: bfloat16 [32, 128, 4096], P('head'), may hold values from -0.09375 to 0.09375
- mod_table: float32 [16, 4096], replicated, may hold values from -3 to 3
- clip_level: int32 [64], replicated, may hold values from 0 to 15
- clip_of: int32 [8192], P('ctx'), may hold values from 0 to 63, never falling along the last dimension, each value on 1 to 256 neighbouring positions
- visible: int32 [64, 64], replicated, may hold values from 0 to 1, as said below
Outputs:
- mixed: bfloat16 [8192, 4096], P(('ctx', 'head'))
Inputs may be any that keep to these rules, and one draw needn't show every extreme that they name: visible is 1 on the diagonal and 0 above it. `clip_of`: clip numbers never fall along the tokens; every clip has 1 to 256 tokens and one has exactly 256.
All inputs are finite; a program needn't handle non-finite values.
Results may differ from a plain program's by a relative error of at most 0.02.
The roundings to bfloat16 on the way count: a program that leaves them out, or rounds other values in their place, can miss the bound.
Values may be sent and summed in bfloat16 or wider, within the bound.
No kernel may reach another device: no remote copies, remote signals or barrier semaphores. Data moves between devices by JAX's collectives and lax.ppermute only.
A program may use at most 128 MiB of HBM per device.

v0:
```python
import math

import jax
import jax.numpy as jnp
from jax import lax
from jax.sharding import PartitionSpec as P


def score_block(state_now, kv_block, key_clips, queries, query_vis, score_scale):
    clip_count = query_vis.shape[1]
    clip_ids = lax.broadcasted_iota(jnp.int32, (1, clip_count), 1)
    key_hot = (key_clips[:, None] == clip_ids).astype(jnp.float32)
    allowed = jnp.dot(query_vis, key_hot.T, precision=lax.Precision.HIGHEST) > 0.5
    top_score, totals, summed = state_now
    key_rows = kv_block[:, 0]
    value_rows = kv_block[:, 1]
    scores = (
        jnp.einsum("rhd,khd->hrk", queries, key_rows, preferred_element_type=jnp.float32)
        * score_scale
    )
    masked = jnp.where(allowed[None], scores, -1e30)
    new_top = jnp.maximum(top_score, jnp.max(masked, axis=2))
    weights = jnp.where(allowed[None], jnp.exp(masked - new_top[:, :, None]), 0.0)
    factor = jnp.exp(top_score - new_top)
    totals = totals * factor + jnp.sum(weights, axis=2)
    summed = summed * factor[:, :, None] + jnp.einsum(
        "hrk,khd->hrd", weights.astype(jnp.bfloat16), value_rows, preferred_element_type=jnp.float32
    )
    return (new_top, totals, summed)


def fold_keys(state_now, kv_rows, key_clips, queries, query_vis, score_scale):
    key_count = kv_rows.shape[0]
    block_rows = math.gcd(key_count, 512)

    def one_block(block_index, state_in):
        first_row = block_index * block_rows
        kv_block = lax.dynamic_slice_in_dim(kv_rows, first_row, block_rows, 0)
        clip_block = lax.dynamic_slice_in_dim(key_clips, first_row, block_rows, 0)
        return score_block(state_in, kv_block, clip_block, queries, query_vis, score_scale)

    return lax.fori_loop(0, key_count // block_rows, one_block, state_now)


def per_device(activations, qkv_weight, out_weight, mod_table, clip_level, clip_of, visible):
    heads_here = qkv_weight.shape[2]
    head_size = qkv_weight.shape[3]
    clip_count = visible.shape[0]
    level_count = mod_table.shape[0]
    clip_ids = lax.broadcasted_iota(jnp.int32, (1, clip_count), 1)
    level_ids = lax.broadcasted_iota(jnp.int32, (1, level_count), 1)
    tok_hot = clip_of[:, None] == clip_ids
    level_rows = jnp.sum(jnp.where(tok_hot, clip_level[None, :], 0), axis=1)
    level_hot = (level_rows[:, None] == level_ids).astype(jnp.float32)
    modulation = jnp.dot(level_hot, mod_table, precision=lax.Precision.HIGHEST)
    moduled = (activations.astype(jnp.float32) * (1.0 + modulation)).astype(jnp.bfloat16)
    qkv = jnp.einsum(
        "td,dchk->tchk", moduled, qkv_weight, preferred_element_type=jnp.float32
    ).astype(jnp.bfloat16)
    queries = qkv[:, 0]
    kv_local = qkv[:, 1:3]
    query_count = queries.shape[0]
    query_hot = (clip_of[:, None] == clip_ids).astype(jnp.float32)
    query_vis = jnp.dot(query_hot, visible.astype(jnp.float32), precision=lax.Precision.HIGHEST)
    score_scale = 1.0 / jnp.sqrt(jnp.float32(head_size))
    initial = (
        jnp.full((heads_here, query_count), -1e30, jnp.float32),
        jnp.zeros((heads_here, query_count), jnp.float32),
        jnp.zeros((heads_here, query_count, head_size), jnp.float32),
    )
    kv_all, clips_all = (
        lax.all_gather(kv_local, "ctx", axis=0, tiled=True),
        lax.all_gather(clip_of, "ctx", axis=0, tiled=True),
    )
    final = fold_keys(initial, kv_all, clips_all, queries, query_vis, score_scale)
    attended = (final[2] / final[1][:, :, None]).astype(jnp.bfloat16)
    attended_rows = jnp.transpose(attended, (1, 0, 2))
    return lax.psum_scatter(
        jnp.einsum(
            "rhd,hdo->ro", attended_rows, out_weight, preferred_element_type=jnp.float32
        ).astype(jnp.bfloat16),
        "head",
        scatter_dimension=0,
        tiled=True,
    )


def solution(mesh):
    placed = (
        P("ctx", None),
        P(None, None, "head", None),
        P("head", None, None),
        P(),
        P(),
        P("ctx"),
        P(),
    )
    return jax.shard_map(
        per_device, mesh=mesh, in_specs=placed, out_specs=P(("ctx", "head"), None), check_vma=False
    )
```

profile of v0, /device:TPU:6, one launch (start us, length us, event | category | flops | bytes accessed | tf_op | source)
XLA Modules:
  0.0 363.2 jit_solution(15202667989823776024)
XLA Ops:
  7.5 5.6 %fusion.20 = bf16[512,4096,1,1]{1,0,3,2:T(8,128)(2,1)S(1)} fusion(f32[16,4096]{1,0:T(8,128)S(1)} %copy-done, bf16[512,4096]{1,0:T(8,128)(2,1)} %param.9, s32[512]{0:T(512)S(1)} %select_reduce_fusion), kind=kOutput, calls=%fused_computation.29 | convolution fusion | flops 411049984 | bytes 8652800 | tf_op jit(solution)/shard_map/dot_general | solution.py:55
  13.1 10.1 %fusion.21 = bf16[512,3,4,128]{3,0,2,1:T(8,128)(2,1)S(1)} fusion(bf16[512,4096,1,1]{1,0,3,2:T(8,128)(2,1)S(1)} %fusion.20, bf16[4096,3,4,128]{3,2,1,0:T(4,128)(2,1)} %param.10), kind=kOutput, calls=%fused_computation.30 | convolution fusion | flops 6443237376 | bytes 18350080 | tf_op jit(solution)/shard_map/td,dchk->tchk/dot_general | solution.py:57
  24.4 21.4 %all-gather = s32[16,1,512]{2,1,0:T(1,128)S(1)} all-gather(s32[1,1,512]{2,1,0:T(1,128)S(1)} %bitcast.58), channel_id=1, replica_groups=mesh['ctx'=16,'head'=8] {'ctx'}, dimensions={0}, use_global_device_ids=true | all-gather | bytes 34816 | tf_op jit(solution)/shard_map/all_gather | solution.py:73
  46.3 88.5 %all-gather.3.cloned.1.call-done = bf16[8192,2,4,128]{3,0,2,1:T(8,128)(2,1)} async-done(((bf16[512,2,4,128]{3,0,2,1:T(8,128)(2,1)}), bf16[8192,2,4,128]{3,0,2,1:T(8,128)(2,1)}) %all-gather.3.cloned.1.call-update) | async-done | bytes 16777232 | tf_op jit(solution)/shard_map/all_gather | solution.py:72
  134.8 123.4 %while.18 = (s32[]{:T(128)}, f32[4,512]{1,0:T(4,128)S(1)}, f32[4,512]{1,0:T(4,128)S(1)}, f32[4,512,128]{2,1,0:T(8,128)}, s32[8192]{0:T(1024)S(1)}, /*index=5*/f3...) while((s32[]{:T(128)}, f32[4,512]{1,0:T(4,128)S(1)}, ...), condition=%wide.region_4.5_spmd.clone, body=%wide.region_1.4_spmd.clone.sunk | while | flops 752920576 | bytes 25958676 | solution.py:42
  135.5 2.0 fusion.46
  138.6 2.9 fusion.49
  146.3 2.9 fusion.49
  154.1 2.9 fusion.49
  161.8 2.9 fusion.49
  169.5 2.9 fusion.49
  177.2 2.9 fusion.49
  184.9 2.9 fusion.49
  192.6 2.9 fusion.49
  200.3 2.9 fusion.49
  208.1 2.9 fusion.49
  215.8 2.9 fusion.49
  223.5 2.9 fusion.49
  231.2 2.9 fusion.49
  238.9 2.9 fusion.49
  246.6 2.9 fusion.49
  254.3 2.9 fusion.49
  258.2 6.9 %bitcast_convert_fusion = bf16[512,4096]{1,0:T(8,128)(2,1)} fusion(bf16[4,128,4096]{2,1,0:T(8,128)(2,1)} %param.11, f32[4,512,128]{2,1,0:T(8,128)} %get-tuple-element.145, f32[4,512]{1,0:T(4,128)S(1)} %get-tuple-element.146), kind=kOutput, calls=%fused_computation.27 | convolution fusion | flops 2150105088 | bytes 9445376 | tf_op jit(solution)/shard_map/rhd,hdo->ro/dot_general | solution.py:79
  265.1 91.3 %reduce-scatter.2.cloned.1.call-done = bf16[64,4096]{1,0:T(8,128)(2,1)} async-done(((bf16[512,4096]{1,0:T(8,128)(2,1)}), bf16[64,4096]{1,0:T(8,128)(2,1)}) %reduce-scatter.2.cloned.1.call-update) | async-done | bytes 524304 | tf_op jit(solution)/shard_map/reduce_scatter | solution.py:78
  (192 shorter events, 77.1 us)
Async XLA Ops:
  6.5 1.0 copy-start
  6.5 128.2 %all-gather.3.cloned.1.call-start = ((), (), s32[]{:S(2)}) async-start(), calls=%async_computation.1 | async-start | bytes 17825792 | tf_op jit(solution)/shard_map/all_gather | solution.py:72
  13.1 11.3 %copy-start.2 = (s32[512]{0:T(512)S(1)}, s32[512]{0:T(512)}, u32[]{:S(2)}) copy-start(s32[512]{0:T(512)} %param.14) | copy-start | bytes 6148
  13.1 32.8 %copy-start.1 = (s32[64,64]{1,0:T(8,128)S(1)}, s32[64,64]{1,0:T(8,128)}, u32[]{:S(2)}) copy-start(s32[64,64]{1,0:T(8,128)} %param.15) | copy-start | bytes 49156
  24.3 332.0 %reduce-scatter.2.cloned.1.call-start = ((), (), s32[]{:S(2)}) async-start(), calls=%async_computation.2 | async-start | bytes 4718592 | tf_op jit(solution)/shard_map/reduce_scatter | solution.py:78
  135.5 3.1 copy-start.3
  141.5 1.0 copy-start.4
  143.2 3.1 copy-start.3
  149.2 1.0 copy-start.4
  150.9 3.1 copy-start.3
  158.7 3.1 copy-start.3
  164.6 1.0 copy-start.4
  166.4 3.1 copy-start.3
  174.1 3.1 copy-start.3
  181.8 3.1 copy-start.3
  189.5 3.1 copy-start.3
  197.2 3.1 copy-start.3
  204.9 3.1 copy-start.3
  212.7 3.1 copy-start.3
  220.4 3.1 copy-start.3
  228.1 3.1 copy-start.3
  235.8 3.1 copy-start.3
  243.5 3.1 copy-start.3
  251.2 3.1 copy-start.3
  (13 other events, 12.7 us)
Sparse Core Ops, SparseCore 0:
  24.5 110.2 all-gather.2
  265.2 91.1 reduce-scatter.1
where the time goes:
time: 365 us; the launch traced here: 363 us
  waiting for transfers between devices  180 us (49%)
  matrix products  112 us (31%)
  blocking collectives  21.4 us (6%)
  local copies, waits for them, and re-layouts  17.9 us (5%)
  other arithmetic  17.9 us (5%)
  between operations  13.5 us (4%)
    reduce_scatter x1, waiting for transfers between devices, per_device(): lax.psum_scatter(jnp.einsum('rhd,hdo->ro', attended_rows, out_weight, pre...  91.3 us
    all_gather x1, waiting for transfers between devices, per_device(): lax.all_gather(kv_local, 'ctx', axis=0, tiled=True)  88.5 us
    dot_general x16, matrix products, score_block(): jnp.einsum('hrk,khd->hrd', weights.astype(jnp.bfloat16), value_rows, pref...  45.8 us
    dot_general x16, matrix products, score_block(): jnp.einsum('rhd,khd->hrk', queries, key_rows, preferred_element_type=jnp....  32.2 us
    all_gather x1, blocking collectives, per_device(): lax.all_gather(clip_of, 'ctx', axis=0, tiled=True)  21.4 us
    reduce_sum x16, other arithmetic, score_block(): totals = totals * factor + jnp.sum(weights, axis=2)  16.6 us
    while x80, local copies, waits for them, and re-layouts  15.5 us
    dot_general x16, matrix products, score_block(): jnp.dot(query_vis, key_hot.T, precision=lax.Precision.HIGHEST) > 0.5  10.6 us
  transfers between devices with their start and end apart: 2, of which 2 were waited for; matrix products, arithmetic and copies ran while one was open for 0% of the time, Pallas kernels for 0%

commit v1 on v0

v1 whole, which is shorter than its diff:
```python
import functools
import math

import jax
import numpy as np
import jax.numpy as jnp
from jax import lax
from jax.experimental import pallas as pl
from jax.experimental.pallas import tpu as pltpu
from jax.sharding import PartitionSpec as P


def attn_kernel(qvis_ref, q_ref, k_ref, v_ref, kh_ref, o_ref, m_sc, l_sc, acc_sc, bias_sc, *, scale, nsteps):
    j = pl.program_id(0)
    h = pl.program_id(1)

    @pl.when((j == 0) & (h == 0))
    def _():
        m_sc[...] = jnp.full(m_sc.shape, -1e30, jnp.float32)
        l_sc[...] = jnp.zeros(l_sc.shape, jnp.float32)
        acc_sc[...] = jnp.zeros(acc_sc.shape, jnp.float32)

    @pl.when(h == 0)
    def _():
        allowed = jnp.dot(qvis_ref[...], kh_ref[...], preferred_element_type=jnp.float32)
        bias_sc[...] = jnp.where(allowed > 0.5, 0.0, -jnp.inf).astype(jnp.float32)

    q = q_ref[h]
    k = k_ref[...]
    v = v_ref[...]
    s = lax.dot_general(q, k, (((1,), (1,)), ((), ())), preferred_element_type=jnp.float32)
    s = s * scale + bias_sc[...]
    m_old = m_sc[h]
    m_new = jnp.maximum(m_old, jnp.max(s, axis=1, keepdims=True))
    p = jnp.exp(s - m_new)
    alpha = jnp.exp(m_old - m_new)
    l_sc[h] = l_sc[h] * alpha + jnp.sum(p, axis=1, keepdims=True)
    acc_sc[h] = acc_sc[h] * alpha + jnp.dot(p.astype(jnp.bfloat16), v, preferred_element_type=jnp.float32)
    m_sc[h] = m_new

    @pl.when(j == nsteps - 1)
    def _():
        out = (acc_sc[h] / l_sc[h]).astype(o_ref.dtype)
        col = pl.multiple_of(h * q_ref.shape[2], q_ref.shape[2])
        o_ref[:, pl.ds(col, q_ref.shape[2])] = out


def flash_attention(qvis, q, kv_all, key_hot, scale):
    heads, nq, hd = q.shape
    sources, _, _, tok, _ = kv_all.shape
    clip_count = qvis.shape[1]
    bk = math.gcd(tok, 512)
    sub = tok // bk
    nsteps = sources * sub
    kernel = functools.partial(attn_kernel, scale=scale, nsteps=nsteps)
    flops = 4 * heads * nq * sources * tok * hd + 2 * nq * clip_count * sources * tok
    cost = pl.CostEstimate(
        flops=flops,
        transcendentals=heads * nq * sources * tok,
        bytes_accessed=kv_all.size * 2 + q.size * 2 + nq * heads * hd * 2,
    )
    return pl.pallas_call(
        kernel,
        grid=(nsteps, heads),
        in_specs=[
            pl.BlockSpec((nq, clip_count), lambda j, h: (0, 0)),
            pl.BlockSpec((heads, nq, hd), lambda j, h: (0, 0, 0)),
            pl.BlockSpec((None, None, None, bk, hd), lambda j, h: (j // sub, 0, h, j % sub, 0)),
            pl.BlockSpec((None, None, None, bk, hd), lambda j, h: (j // sub, 1, h, j % sub, 0)),
            pl.BlockSpec((None, clip_count, bk), lambda j, h: (j // sub, 0, j % sub)),
        ],
        out_specs=pl.BlockSpec((nq, heads * hd), lambda j, h: (0, 0)),
        out_shape=jax.ShapeDtypeStruct((nq, heads * hd), jnp.bfloat16),
        scratch_shapes=[
            pltpu.VMEM((heads, nq, 1), jnp.float32),
            pltpu.VMEM((heads, nq, 1), jnp.float32),
            pltpu.VMEM((heads, nq, hd), jnp.float32),
            pltpu.VMEM((nq, bk), jnp.float32),
        ],
        compiler_params=pltpu.CompilerParams(dimension_semantics=("arbitrary", "arbitrary")),
        cost_estimate=cost,
    )(qvis, q, kv_all, kv_all, key_hot)


def per_device(activations, qkv_weight, out_weight, mod_table, clip_level, clip_of, visible):
    heads_here = qkv_weight.shape[2]
    head_size = qkv_weight.shape[3]
    clip_count = visible.shape[0]
    level_count = mod_table.shape[0]
    clip_ids = lax.broadcasted_iota(jnp.int32, (1, clip_count), 1)
    level_ids = lax.broadcasted_iota(jnp.int32, (1, level_count), 1)
    tok_hot = clip_of[:, None] == clip_ids
    level_rows = jnp.sum(jnp.where(tok_hot, clip_level[None, :], 0), axis=1)
    level_hot = (level_rows[:, None] == level_ids).astype(jnp.float32)
    modulation = jnp.dot(level_hot, mod_table, precision=lax.Precision.HIGHEST)
    moduled = (activations.astype(jnp.float32) * (1.0 + modulation)).astype(jnp.bfloat16)
    qkv = jnp.einsum(
        "td,dchk->chtk", moduled, qkv_weight, preferred_element_type=jnp.float32
    ).astype(jnp.bfloat16)
    queries = qkv[0]
    kv_local = qkv[1:3]
    query_hot = tok_hot.astype(jnp.float32)
    qvis = jnp.dot(query_hot, visible.astype(jnp.float32), precision=lax.Precision.HIGHEST).astype(jnp.bfloat16)
    score_scale = float(np.float32(1.0) / np.sqrt(np.float32(head_size)))
    kv_all = lax.all_gather(kv_local, "ctx", axis=0)
    clips_all = lax.all_gather(clip_of, "ctx", axis=0)
    key_hot = (clips_all[:, None, :] == clip_ids[0][None, :, None]).astype(jnp.bfloat16)
    attended = flash_attention(qvis, queries, kv_all, key_hot, score_scale)
    ow = out_weight.reshape(heads_here * head_size, out_weight.shape[2])
    mixed = jnp.dot(attended, ow, preferred_element_type=jnp.float32).astype(jnp.bfloat16)
    return lax.psum_scatter(mixed, "head", scatter_dimension=0, tiled=True)


def solution(mesh):
    placed = (
        P("ctx", None),
        P(None, None, "head", None),
        P("head", None, None),
        P(),
        P(),
        P("ctx"),
        P(),
    )
    return jax.shard_map(
        per_device, mesh=mesh, in_specs=placed, out_specs=P(("ctx", "head"), None), check_vma=False
    )
```

time: 365 us -> 333 us (0.912)
  Pallas kernels: 0 us -> 92.7 us
  matrix products: 112 us -> 22.6 us
  other arithmetic: 17.9 us -> 2.16 us
  local copies, waits for them, and re-layouts: 17.9 us -> 2.83 us
    pallas_call x0 -> x1, Pallas kernels: none -> 92.7 us  [flash_attention(): pl.pallas_call(kernel, grid=(nsteps, heads), in_specs=[pl.BlockSpec((nq,...]
    dot_general x50 -> x2, matrix products: 106 us -> 16.7 us  [the longest x1 10.1 us: per_device(): jnp.einsum('td,dchk->chtk', moduled, qkv_weight, preferred_element_type=j...]
    reduce_sum x16 -> x0, other arithmetic: 16.6 us -> none  [score_block(): totals = totals * factor + jnp.sum(weights, axis=2)]
    while x80 -> x0, local copies, waits for them, and re-layouts: 15.5 us -> none
  transfers between devices with their start and end apart: 2 -> 2, of which waited for: 2 -> 2; matrix products, arithmetic and copies ran while one was open for 0% -> 1% of each run, Pallas kernels for 0% -> 0%
where the time goes in v1:
time: 333 us; the launch traced here: 332 us
  waiting for transfers between devices  177 us (53%)
  Pallas kernels  92.7 us (28%)
  matrix products  22.6 us (7%)
  blocking collectives  21.2 us (6%)
  between operations  13.5 us (4%)
    pallas_call x1, Pallas kernels, flash_attention(): pl.pallas_call(kernel, grid=(nsteps, heads), in_specs=[pl.BlockSpec((nq,...  92.7 us
    reduce_scatter x1, waiting for transfers between devices, per_device(): return lax.psum_scatter(mixed, 'head', scatter_dimension=0, tiled=True)  91.3 us
    all_gather x1, waiting for transfers between devices, per_device(): kv_all = lax.all_gather(kv_local, 'ctx', axis=0)  85.9 us
    all_gather x1, blocking collectives, per_device(): clips_all = lax.all_gather(clip_of, 'ctx', axis=0)  21.2 us
    dot_general x1, matrix products, per_device(): jnp.einsum('td,dchk->chtk', moduled, qkv_weight, preferred_element_type=j...  10.1 us
  transfers between devices with their start and end apart: 2, of which 2 were waited for; matrix products, arithmetic and copies ran while one was open for 1% of the time, Pallas kernels for 0%

profile of v1, /device:TPU:6, one launch (start us, length us, event | category | flops | bytes accessed | tf_op | source)
XLA Modules:
  0.0 332.3 jit_solution(12735307918677824342)
XLA Ops:
  6.5 0.0 copy-start
  6.5 0.0 all-gather.5.cloned.1.call-start
  6.5 0.8 select_reduce_fusion
  7.4 0.1 copy-done
  7.5 5.6 %fusion.2 = bf16[512,4096,1,1]{1,0,3,2:T(8,128)(2,1)S(1)} fusion(f32[16,4096]{1,0:T(8,128)S(1)} %copy-done, bf16[512,4096]{1,0:T(8,128)(2,1)} %param.7, s32[512]{0:T(512)S(1)} %select_reduce_fusion), kind=kOutput, calls=%fused_computation.4 | convolution fusion | flops 411049984 | bytes 8652800 | tf_op jit(solution)/shard_map/dot_general | solution.py:95
  13.1 0.0 copy-start.1
  13.1 0.0 copy-start.2
  13.1 10.1 %fusion.7 = bf16[3,4,512,128]{3,2,1,0:T(8,128)(2,1)S(1)} fusion(bf16[512,4096,1,1]{1,0,3,2:T(8,128)(2,1)S(1)} %fusion.2, bf16[4096,3,4,128]{3,2,1,0:T(4,128)(2,1)} %param.8), kind=kOutput, calls=%fused_computation.8 | convolution fusion | flops 6443237376 | bytes 18350080 | tf_op jit(solution)/shard_map/td,dchk->chtk/dot_general | solution.py:97
  23.2 1.1 slice.9
  24.3 0.0 all-gather.5.cloned.1.call-update
  24.3 0.0 reduce-scatter.2.cloned.1.call-start
  24.4 0.0 copy-done.1
  24.4 0.0 copy-done.2
  24.4 0.3 convolution_convert_fusion.1
  24.7 0.8 copy.13.qvis_ref
  25.4 21.2 %all-gather.2 = s32[16,1,512]{2,1,0:T(1,128)S(1)} all-gather(s32[1,1,512]{2,1,0:T(1,128)S(1)} %bitcast.21), channel_id=3, replica_groups=mesh['ctx'=16,'head'=8] {'ctx'}, dimensions={0}, use_global_device_ids=true | all-gather | bytes 34816 | tf_op jit(solution)/shard_map/all_gather | solution.py:106
  46.7 0.8 slice_bitcast_fusion.q_ref
  47.5 1.3 fusion.3.kh_ref
  48.8 85.9 %all-gather.5.cloned.1.call-done = bf16[32,4,512,128]{3,2,1,0:T(8,128)(2,1)} async-done(((bf16[2,4,512,128]{3,2,1,0:T(8,128)(2,1)}), bf16[32,4,512,128]{3,2,1,0:T(8,128)(2,1)}) %all-gather.5.cloned.1.call-update) | async-done | bytes 16777232 | tf_op jit(solution)/shard_map/all_gather | solution.py:105
  134.8 92.7 %shard_map.73 = bf16[512,512]{1,0:T(8,128)(2,1)} custom-call(bf16[512,64]{1,0:T(8,128)(2,1)} %copy.13.qvis_ref, bf16[4,512,128]{2,1,0:T(8,128)(2,1)} %slice_bitcast_fusion.q_ref, bf16[16,2,4,512,128]{4,3,2,1,0:T(8,128)(2,1)} %bitcast.18, bf16[16,2,4,512,128]{4,3,2,1,0:T(8,128)(2,1)} %bitcast.19, bf16[16,64,512]{2,1,0:T(8,128)(2,1)} %fusion.3.kh_ref), custom_call_target="tpu_custom_call" | custom-call | flops 9126805504 | bytes 17825792 | tf_op jit(solution)/shard_map/pallas_call | solution.py:62
  227.4 6.6 %convolution_convert_fusion = bf16[512,4096]{1,0:T(8,128)(2,1)} fusion(bf16[512,512]{1,0:T(8,128)(2,1)} %shard_map.73, bf16[512,4096]{1,0:T(8,128)(2,1)} %bitcast.22), kind=kOutput, calls=%fused_computation.3 | convolution fusion | flops 2149580800 | bytes 8912896 | tf_op jit(solution)/shard_map/dot_general | solution.py:110
  234.1 0.0 reduce-scatter.2.cloned.1.call-update
  234.1 91.3 %reduce-scatter.2.cloned.1.call-done = bf16[64,4096]{1,0:T(8,128)(2,1)} async-done(((bf16[512,4096]{1,0:T(8,128)(2,1)}), bf16[64,4096]{1,0:T(8,128)(2,1)}) %reduce-scatter.2.cloned.1.call-update) | async-done | bytes 524304 | tf_op jit(solution)/shard_map/reduce_scatter | solution.py:111
  (1 shorter events, 0.0 us)
Async XLA Ops:
  6.5 1.0 copy-start
  6.5 128.2 %all-gather.5.cloned.1.call-start = ((), (), s32[]{:S(2)}) async-start(), calls=%async_computation.2 | async-start | bytes 17825792 | tf_op jit(solution)/shard_map/all_gather | solution.py:105
  13.1 11.3 %copy-start.1 = (s32[64,64]{1,0:T(8,128)S(1)}, s32[64,64]{1,0:T(8,128)}, u32[]{:S(2)}) copy-start(s32[64,64]{1,0:T(8,128)} %param.13) | copy-start | bytes 49156
  13.1 11.3 %copy-start.2 = (s32[512]{0:T(512)S(1)}, s32[512]{0:T(512)}, u32[]{:S(2)}) copy-start(s32[512]{0:T(512)} %param.12) | copy-start | bytes 6148
  24.3 301.1 %reduce-scatter.2.cloned.1.call-start = ((), (), s32[]{:S(2)}) async-start(), calls=%async_computation.1 | async-start | bytes 4718592 | tf_op jit(solution)/shard_map/reduce_scatter | solution.py:111
Sparse Core Ops, SparseCore 0:
  24.5 110.2 all-gather.4
  234.2 91.1 reduce-scatter.1

commit v2 on v1

--- a/solution.py
+++ b/solution.py
@@ -108,7 +108,10 @@
     attended = flash_attention(qvis, queries, kv_all, key_hot, score_scale)
     ow = out_weight.reshape(heads_here * head_size, out_weight.shape[2])
     mixed = jnp.dot(attended, ow, preferred_element_type=jnp.float32).astype(jnp.bfloat16)
-    return lax.psum_scatter(mixed, "head", scatter_dimension=0, tiled=True)
+    groups = lax.axis_size("head")
+    parts = mixed.reshape(groups, mixed.shape[0] // groups, mixed.shape[1])
+    parts = lax.all_to_all(parts, "head", 0, 0)
+    return jnp.sum(parts.astype(jnp.float32), axis=0).astype(jnp.bfloat16)
 
 
 def solution(mesh):

time: 333 us -> 299 us (0.90)
  waiting for transfers between devices: 177 us -> 86 us
  blocking collectives: 21.2 us -> 75.4 us
  other arithmetic: 2.16 us -> 6.02 us
    reduce_scatter x1 -> x0, waiting for transfers between devices: 91.3 us -> none  [per_device(): return lax.psum_scatter(mixed, 'head', scatter_dimension=0, tiled=True)]
    all_to_all x0 -> x1, blocking collectives: none -> 54.2 us  [per_device(): parts = lax.all_to_all(parts, 'head', 0, 0)]
    reduce_sum x0 -> x1, other arithmetic: none -> 3.84 us  [per_device(): return jnp.sum(parts.astype(jnp.float32), axis=0).astype(jnp.bfloat16)]
  transfers between devices with their start and end apart: 2 -> 1, of which waited for: 2 -> 1; matrix products, arithmetic and copies ran while one was open for 1% -> 1% of each run, Pallas kernels for 0% -> 0%
where the time goes in v2:
time: 299 us; the launch traced here: 297 us
  Pallas kernels  92.7 us (31%)
  waiting for transfers between devices  86 us (29%)
  blocking collectives  75.4 us (25%)
  matrix products  20.6 us (7%)
  between operations  13.5 us (5%)
  other arithmetic  6.02 us (2%)
    pallas_call x1, Pallas kernels, flash_attention(): pl.pallas_call(kernel, grid=(nsteps, heads), in_specs=[pl.BlockSpec((nq,...  92.7 us
    all_gather x1, waiting for transfers between devices, per_device(): kv_all = lax.all_gather(kv_local, 'ctx', axis=0)  86 us
    all_to_all x1, blocking collectives, per_device(): parts = lax.all_to_all(parts, 'head', 0, 0)  54.2 us
    all_gather x1, blocking collectives, per_device(): clips_all = lax.all_gather(clip_of, 'ctx', axis=0)  21.2 us
    dot_general x1, matrix products, per_device(): jnp.einsum('td,dchk->chtk', moduled, qkv_weight, preferred_element_type=j...  10.1 us
  transfers between devices with their start and end apart: 1, of which 1 were waited for; matrix products, arithmetic and copies ran while one was open for 1% of the time, Pallas kernels for 0%

profile of v2, /device:TPU:6, one launch (start us, length us, event | category | flops | bytes accessed | tf_op | source)
XLA Modules:
  0.0 297.0 jit_solution(16178945979250511270)
XLA Ops:
  6.5 0.0 copy-start
  6.5 0.0 all-gather.5.cloned.1.call-start
  6.5 0.8 select_reduce_fusion
  7.4 0.1 copy-done
  7.5 5.6 %fusion.2 = bf16[512,4096,1,1]{1,0,3,2:T(8,128)(2,1)S(1)} fusion(f32[16,4096]{1,0:T(8,128)S(1)} %copy-done, bf16[512,4096]{1,0:T(8,128)(2,1)} %param.7, s32[512]{0:T(512)S(1)} %select_reduce_fusion), kind=kOutput, calls=%fused_computation.4 | convolution fusion | flops 411049984 | bytes 8652800 | tf_op jit(solution)/shard_map/dot_general | solution.py:95
  13.1 0.0 copy-start.1
  13.1 0.0 copy-start.2
  13.1 10.1 %fusion.7 = bf16[3,4,512,128]{3,2,1,0:T(8,128)(2,1)S(1)} fusion(bf16[512,4096,1,1]{1,0,3,2:T(8,128)(2,1)S(1)} %fusion.2, bf16[4096,3,4,128]{3,2,1,0:T(4,128)(2,1)} %param.8), kind=kOutput, calls=%fused_computation.8 | convolution fusion | flops 6443237376 | bytes 18350080 | tf_op jit(solution)/shard_map/td,dchk->chtk/dot_general | solution.py:97
  23.2 1.1 slice.9
  24.3 0.0 all-gather.5.cloned.1.call-update
  24.4 0.0 copy-done.1
  24.4 0.0 copy-done.2
  24.4 0.3 convolution_convert_fusion.1
  24.6 0.8 copy.13.qvis_ref
  25.4 21.2 %all-gather.2 = s32[16,1,512]{2,1,0:T(1,128)S(1)} all-gather(s32[1,1,512]{2,1,0:T(1,128)S(1)} %bitcast.23), channel_id=3, replica_groups=mesh['ctx'=16,'head'=8] {'ctx'}, dimensions={0}, use_global_device_ids=true | all-gather | bytes 34816 | tf_op jit(solution)/shard_map/all_gather | solution.py:106
  46.6 0.8 slice_bitcast_fusion.q_ref
  47.5 1.3 fusion.3.kh_ref
  48.8 86.0 %all-gather.5.cloned.1.call-done = bf16[32,4,512,128]{3,2,1,0:T(8,128)(2,1)} async-done(((bf16[2,4,512,128]{3,2,1,0:T(8,128)(2,1)}), bf16[32,4,512,128]{3,2,1,0:T(8,128)(2,1)}) %all-gather.5.cloned.1.call-update) | async-done | bytes 16777232 | tf_op jit(solution)/shard_map/all_gather | solution.py:105
  134.8 92.7 %shard_map.73 = bf16[512,512]{1,0:T(8,128)(2,1)} custom-call(bf16[512,64]{1,0:T(8,128)(2,1)} %copy.13.qvis_ref, bf16[4,512,128]{2,1,0:T(8,128)(2,1)} %slice_bitcast_fusion.q_ref, bf16[16,2,4,512,128]{4,3,2,1,0:T(8,128)(2,1)} %bitcast.19, bf16[16,2,4,512,128]{4,3,2,1,0:T(8,128)(2,1)} %bitcast.20, bf16[16,64,512]{2,1,0:T(8,128)(2,1)} %fusion.3.kh_ref), custom_call_target="tpu_custom_call" | custom-call | flops 9126805504 | bytes 17825792 | tf_op jit(solution)/shard_map/pallas_call | solution.py:62
  227.5 4.7 %convolution_convert_fusion = bf16[512,4096]{1,0:T(8,128)(2,1)S(1)} fusion(bf16[512,512]{1,0:T(8,128)(2,1)} %shard_map.73, bf16[512,4096]{1,0:T(8,128)(2,1)} %bitcast.24), kind=kOutput, calls=%fused_computation.3 | convolution fusion | flops 2149580800 | bytes 8912896 | tf_op jit(solution)/shard_map/dot_general | solution.py:110
  232.2 54.2 %all_to_all.5 = bf16[8,64,4096]{2,1,0:T(8,128)(2,1)} all-to-all(bf16[8,64,4096]{2,1,0:T(8,128)(2,1)S(1)} %bitcast.21), channel_id=1, replica_groups=mesh['ctx'=16,'head'=8] {'head'}, dimensions={0} | all-to-all | bytes 8388608 | tf_op jit(solution)/shard_map/all_to_all | solution.py:113
  286.3 3.8 %reduce_sum.22 = bf16[64,4096]{1,0:T(8,128)(2,1)} reduce(bf16[8,64,4096]{2,1,0:T(8,128)(2,1)} %all_to_all.5, bf16[]{:T(256)} %constant.6.clone.1), dimensions={0}, to_apply=%region_1.2 | reduce | flops 1835008 | bytes 4718594 | tf_op jit(solution)/shard_map/reduce_sum | solution.py:114
  (1 shorter events, 0.0 us)
Async XLA Ops:
  6.5 1.0 copy-start
  6.5 128.2 %all-gather.5.cloned.1.call-start = ((), (), s32[]{:S(2)}) async-start(), calls=%async_computation.1 | async-start | bytes 17825792 | tf_op jit(solution)/shard_map/all_gather | solution.py:105
  13.1 11.3 %copy-start.1 = (s32[64,64]{1,0:T(8,128)S(1)}, s32[64,64]{1,0:T(8,128)}, u32[]{:S(2)}) copy-start(s32[64,64]{1,0:T(8,128)} %param.13) | copy-start | bytes 49156
  13.1 11.3 %copy-start.2 = (s32[512]{0:T(512)S(1)}, s32[512]{0:T(512)}, u32[]{:S(2)}) copy-start(s32[512]{0:T(512)} %param.12) | copy-start | bytes 6148
Sparse Core Ops, SparseCore 0:
  24.5 110.2 all-gather.4

commit v3 on v2

--- a/solution.py
+++ b/solution.py
@@ -10,39 +10,37 @@
 from jax.sharding import PartitionSpec as P
 
 
-def attn_kernel(qvis_ref, q_ref, k_ref, v_ref, kh_ref, o_ref, m_sc, l_sc, acc_sc, bias_sc, *, scale, nsteps):
+def attn_kernel(qvis_ref, q_ref, kv_ref, kh_ref, o_ref, m_sc, l_sc, acc_sc, *, scale, nsteps, heads):
     j = pl.program_id(0)
-    h = pl.program_id(1)
+    lanes = m_sc.shape[2]
 
-    @pl.when((j == 0) & (h == 0))
+    @pl.when(j == 0)
     def _():
         m_sc[...] = jnp.full(m_sc.shape, -1e30, jnp.float32)
         l_sc[...] = jnp.zeros(l_sc.shape, jnp.float32)
         acc_sc[...] = jnp.zeros(acc_sc.shape, jnp.float32)
 
-    @pl.when(h == 0)
-    def _():
-        allowed = jnp.dot(qvis_ref[...], kh_ref[...], preferred_element_type=jnp.float32)
-        bias_sc[...] = jnp.where(allowed > 0.5, 0.0, -jnp.inf).astype(jnp.float32)
-
-    q = q_ref[h]
-    k = k_ref[...]
-    v = v_ref[...]
-    s = lax.dot_general(q, k, (((1,), (1,)), ((), ())), preferred_element_type=jnp.float32)
-    s = s * scale + bias_sc[...]
-    m_old = m_sc[h]
-    m_new = jnp.maximum(m_old, jnp.max(s, axis=1, keepdims=True))
-    p = jnp.exp(s - m_new)
-    alpha = jnp.exp(m_old - m_new)
-    l_sc[h] = l_sc[h] * alpha + jnp.sum(p, axis=1, keepdims=True)
-    acc_sc[h] = acc_sc[h] * alpha + jnp.dot(p.astype(jnp.bfloat16), v, preferred_element_type=jnp.float32)
-    m_sc[h] = m_new
+    allowed = jnp.dot(qvis_ref[...], kh_ref[...], preferred_element_type=jnp.float32)
+    bias = jnp.where(allowed > 0.5, 0.0, -jnp.inf).astype(jnp.float32)
+    bk = bias.shape[1]
+    for h in range(heads):
+        s = lax.dot_general(q_ref[h], kv_ref[0, h], (((1,), (1,)), ((), ())), preferred_element_type=jnp.float32)
+        s = s * scale + bias
+        m_old = m_sc[h]
+        m_new = jnp.maximum(m_old, jnp.max(s, axis=1, keepdims=True))
+        p = jnp.exp(s - jnp.tile(m_new, (1, bk // lanes)))
+        alpha = jnp.exp(m_old - m_new)
+        l_sc[h] = l_sc[h] * alpha + jnp.sum(p, axis=1, keepdims=True)
+        acc_sc[h] = acc_sc[h] * alpha + jnp.dot(
+            p.astype(jnp.bfloat16), kv_ref[1, h], preferred_element_type=jnp.float32
+        )
+        m_sc[h] = m_new
 
     @pl.when(j == nsteps - 1)
     def _():
-        out = (acc_sc[h] / l_sc[h]).astype(o_ref.dtype)
-        col = pl.multiple_of(h * q_ref.shape[2], q_ref.shape[2])
-        o_ref[:, pl.ds(col, q_ref.shape[2])] = out
+        hd = acc_sc.shape[2]
+        for h in range(heads):
+            o_ref[:, h * hd:(h + 1) * hd] = (acc_sc[h] / l_sc[h]).astype(o_ref.dtype)
 
 
 def flash_attention(qvis, q, kv_all, key_hot, scale):
@@ -52,7 +50,7 @@
     bk = math.gcd(tok, 512)
     sub = tok // bk
     nsteps = sources * sub
-    kernel = functools.partial(attn_kernel, scale=scale, nsteps=nsteps)
+    kernel = functools.partial(attn_kernel, scale=scale, nsteps=nsteps, heads=heads)
     flops = 4 * heads * nq * sources * tok * hd + 2 * nq * clip_count * sources * tok
     cost = pl.CostEstimate(
         flops=flops,
@@ -61,25 +59,23 @@
     )
     return pl.pallas_call(
         kernel,
-        grid=(nsteps, heads),
+        grid=(nsteps,),
         in_specs=[
-            pl.BlockSpec((nq, clip_count), lambda j, h: (0, 0)),
-            pl.BlockSpec((heads, nq, hd), lambda j, h: (0, 0, 0)),
-            pl.BlockSpec((None, None, None, bk, hd), lambda j, h: (j // sub, 0, h, j % sub, 0)),
-            pl.BlockSpec((None, None, None, bk, hd), lambda j, h: (j // sub, 1, h, j % sub, 0)),
-            pl.BlockSpec((None, clip_count, bk), lambda j, h: (j // sub, 0, j % sub)),
+            pl.BlockSpec((nq, clip_count), lambda j: (0, 0)),
+            pl.BlockSpec((heads, nq, hd), lambda j: (0, 0, 0)),
+            pl.BlockSpec((None, 2, heads, bk, hd), lambda j: (j // sub, 0, 0, j % sub, 0)),
+            pl.BlockSpec((None, clip_count, bk), lambda j: (j // sub, 0, j % sub)),
         ],
-        out_specs=pl.BlockSpec((nq, heads * hd), lambda j, h: (0, 0)),
+        out_specs=pl.BlockSpec((nq, heads * hd), lambda j: (0, 0)),
         out_shape=jax.ShapeDtypeStruct((nq, heads * hd), jnp.bfloat16),
         scratch_shapes=[
-            pltpu.VMEM((heads, nq, 1), jnp.float32),
-            pltpu.VMEM((heads, nq, 1), jnp.float32),
+            pltpu.VMEM((heads, nq, 128), jnp.float32),
+            pltpu.VMEM((heads, nq, 128), jnp.float32),
             pltpu.VMEM((heads, nq, hd), jnp.float32),
-            pltpu.VMEM((nq, bk), jnp.float32),
         ],
-        compiler_params=pltpu.CompilerParams(dimension_semantics=("arbitrary", "arbitrary")),
+        compiler_params=pltpu.CompilerParams(dimension_semantics=("arbitrary",)),
         cost_estimate=cost,
-    )(qvis, q, kv_all, kv_all, key_hot)
+    )(qvis, q, kv_all, key_hot)
 
 
 def per_device(activations, qkv_weight, out_weight, mod_table, clip_level, clip_of, visible):

time: 299 us -> 243 us (0.81)
  Pallas kernels: 92.7 us -> 36.8 us
    pallas_call x1, Pallas kernels: 92.7 us -> 36.8 us  [flash_attention(): pl.pallas_call(kernel, grid=(nsteps,), in_specs=[pl.BlockSpec((nq, clip_c...]
where the time goes in v3:
time: 243 us; the launch traced here: 241 us
  waiting for transfers between devices  86 us (35%)
  blocking collectives  75.4 us (31%)
  Pallas kernels  36.8 us (15%)
  matrix products  20.6 us (8%)
  between operations  13.5 us (6%)
  other arithmetic  6.02 us (2%)
  local copies, waits for them, and re-layouts  2.85 us (1%)
    all_gather x1, waiting for transfers between devices, per_device(): kv_all = lax.all_gather(kv_local, 'ctx', axis=0)  86 us
    all_to_all x1, blocking collectives, per_device(): parts = lax.all_to_all(parts, 'head', 0, 0)  54.2 us
    pallas_call x1, Pallas kernels, flash_attention(): pl.pallas_call(kernel, grid=(nsteps,), in_specs=[pl.BlockSpec((nq, clip_c...  36.8 us
    all_gather x1, blocking collectives, per_device(): clips_all = lax.all_gather(clip_of, 'ctx', axis=0)  21.2 us
    dot_general x1, matrix products, per_device(): jnp.einsum('td,dchk->chtk', moduled, qkv_weight, preferred_element_type=j...  10.1 us
    dot_general x1, matrix products, per_device(): modulation = jnp.dot(level_hot, mod_table, precision=lax.Precision.HIGHEST)  5.58 us
  transfers between devices with their start and end apart: 1, of which 1 were waited for; matrix products, arithmetic and copies ran while one was open for 1% of the time, Pallas kernels for 0%

profile of v3, /device:TPU:6, one launch (start us, length us, event | category | flops | bytes accessed | tf_op | source)
XLA Modules:
  0.0 241.1 jit_solution(12235636880489527165)
XLA Ops:
  6.5 0.0 copy-start
  6.5 0.0 all-gather.5.cloned.1.call-start
  6.5 0.8 select_reduce_fusion
  7.4 0.1 copy-done
  7.5 5.6 %fusion.2 = bf16[512,4096,1,1]{1,0,3,2:T(8,128)(2,1)S(1)} fusion(f32[16,4096]{1,0:T(8,128)S(1)} %copy-done, bf16[512,4096]{1,0:T(8,128)(2,1)} %param.7, s32[512]{0:T(512)S(1)} %select_reduce_fusion), kind=kOutput, calls=%fused_computation.4 | convolution fusion | flops 411049984 | bytes 8652800 | tf_op jit(solution)/shard_map/dot_general | solution.py:91
  13.1 0.0 copy-start.1
  13.1 0.0 copy-start.2
  13.1 10.1 %fusion.7 = bf16[3,4,512,128]{3,2,1,0:T(8,128)(2,1)S(1)} fusion(bf16[512,4096,1,1]{1,0,3,2:T(8,128)(2,1)S(1)} %fusion.2, bf16[4096,3,4,128]{3,2,1,0:T(4,128)(2,1)} %param.8), kind=kOutput, calls=%fused_computation.8 | convolution fusion | flops 6443237376 | bytes 18350080 | tf_op jit(solution)/shard_map/td,dchk->chtk/dot_general | solution.py:93
  23.2 1.1 slice.9
  24.3 0.0 all-gather.5.cloned.1.call-update
  24.4 0.0 copy-done.1
  24.4 0.0 copy-done.2
  24.4 0.3 convolution_convert_fusion.1
  24.6 0.8 copy.13.qvis_ref
  25.4 21.2 %all-gather.2 = s32[16,1,512]{2,1,0:T(1,128)S(1)} all-gather(s32[1,1,512]{2,1,0:T(1,128)S(1)} %bitcast.21), channel_id=3, replica_groups=mesh['ctx'=16,'head'=8] {'ctx'}, dimensions={0}, use_global_device_ids=true | all-gather | bytes 34816 | tf_op jit(solution)/shard_map/all_gather | solution.py:102
  46.6 0.8 slice_bitcast_fusion.q_ref
  47.5 1.3 fusion.3.kh_ref
  48.8 86.0 %all-gather.5.cloned.1.call-done = bf16[32,4,512,128]{3,2,1,0:T(8,128)(2,1)} async-done(((bf16[2,4,512,128]{3,2,1,0:T(8,128)(2,1)}), bf16[32,4,512,128]{3,2,1,0:T(8,128)(2,1)}) %all-gather.5.cloned.1.call-update) | async-done | bytes 16777232 | tf_op jit(solution)/shard_map/all_gather | solution.py:101
  134.8 36.8 %shard_map.73 = bf16[512,512]{1,0:T(8,128)(2,1)} custom-call(bf16[512,64]{1,0:T(8,128)(2,1)} %copy.13.qvis_ref, bf16[4,512,128]{2,1,0:T(8,128)(2,1)} %slice_bitcast_fusion.q_ref, bf16[16,2,4,512,128]{4,3,2,1,0:T(8,128)(2,1)} %bitcast.22, bf16[16,64,512]{2,1,0:T(8,128)(2,1)} %fusion.3.kh_ref), custom_call_target="tpu_custom_call" | custom-call | flops 9126805504 | bytes 17825792 | tf_op jit(solution)/shard_map/pallas_call | solution.py:60
  171.5 4.7 %convolution_convert_fusion = bf16[512,4096]{1,0:T(8,128)(2,1)S(1)} fusion(bf16[512,512]{1,0:T(8,128)(2,1)} %shard_map.73, bf16[512,4096]{1,0:T(8,128)(2,1)} %bitcast.23), kind=kOutput, calls=%fused_computation.3 | convolution fusion | flops 2149580800 | bytes 8912896 | tf_op jit(solution)/shard_map/dot_general | solution.py:106
  176.3 54.2 %all_to_all.5 = bf16[8,64,4096]{2,1,0:T(8,128)(2,1)} all-to-all(bf16[8,64,4096]{2,1,0:T(8,128)(2,1)S(1)} %bitcast.19), channel_id=1, replica_groups=mesh['ctx'=16,'head'=8] {'head'}, dimensions={0} | all-to-all | bytes 8388608 | tf_op jit(solution)/shard_map/all_to_all | solution.py:109
  230.4 3.8 %reduce_sum.22 = bf16[64,4096]{1,0:T(8,128)(2,1)} reduce(bf16[8,64,4096]{2,1,0:T(8,128)(2,1)} %all_to_all.5, bf16[]{:T(256)} %constant.6.clone.1), dimensions={0}, to_apply=%region_1.2 | reduce | flops 1835008 | bytes 4718594 | tf_op jit(solution)/shard_map/reduce_sum | solution.py:110
  (1 shorter events, 0.0 us)
Async XLA Ops:
  6.5 1.0 copy-start
  6.5 128.2 %all-gather.5.cloned.1.call-start = ((), (), s32[]{:S(2)}) async-start(), calls=%async_computation.1 | async-start | bytes 17825792 | tf_op jit(solution)/shard_map/all_gather | solution.py:101
  13.1 11.3 %copy-start.1 = (s32[64,64]{1,0:T(8,128)S(1)}, s32[64,64]{1,0:T(8,128)}, u32[]{:S(2)}) copy-start(s32[64,64]{1,0:T(8,128)} %param.13) | copy-start | bytes 49156
  13.1 11.3 %copy-start.2 = (s32[512]{0:T(512)S(1)}, s32[512]{0:T(512)}, u32[]{:S(2)}) copy-start(s32[512]{0:T(512)} %param.12) | copy-start | bytes 6148
Sparse Core Ops, SparseCore 0:
  24.5 110.2 all-gather.4

commit v4 on v3

--- a/solution.py
+++ b/solution.py
@@ -7,7 +7,7 @@
 from jax import lax
 from jax.experimental import pallas as pl
 from jax.experimental.pallas import tpu as pltpu
-from jax.sharding import PartitionSpec as P
+from jax.sharding import Mesh, PartitionSpec as P
 
 
 def attn_kernel(qvis_ref, q_ref, kv_ref, kh_ref, o_ref, m_sc, l_sc, acc_sc, *, scale, nsteps, heads):
@@ -93,17 +93,33 @@
     qkv = jnp.einsum(
         "td,dchk->chtk", moduled, qkv_weight, preferred_element_type=jnp.float32
     ).astype(jnp.bfloat16)
-    queries = qkv[0]
-    kv_local = qkv[1:3]
-    query_hot = tok_hot.astype(jnp.float32)
-    qvis = jnp.dot(query_hot, visible.astype(jnp.float32), precision=lax.Precision.HIGHEST).astype(jnp.bfloat16)
+    core = lax.axis_index("core")
+    half = heads_here // 2
+    swap = [(0, 1), (1, 0)]
+    mine = lax.dynamic_slice_in_dim(qkv, core * half, half, axis=1)
+    other = lax.dynamic_slice_in_dim(qkv, (1 - core) * half, half, axis=1)
+    recv = lax.ppermute(other, "core", swap)
+    clip_recv = lax.ppermute(clip_of, "core", swap)
+    both = jnp.concatenate([mine, recv], axis=2)
+    clip_pair = jnp.concatenate([clip_of, clip_recv])
+    queries = both[0]
+    kv_local = both[1:3]
+    pair_hot = (clip_pair[:, None] == clip_ids).astype(jnp.float32)
+    qvis = jnp.dot(pair_hot, visible.astype(jnp.float32), precision=lax.Precision.HIGHEST).astype(jnp.bfloat16)
     score_scale = float(np.float32(1.0) / np.sqrt(np.float32(head_size)))
-    kv_all = lax.all_gather(kv_local, "ctx", axis=0)
-    clips_all = lax.all_gather(clip_of, "ctx", axis=0)
+    kv_all = lax.all_gather(kv_local, "cx", axis=0)
+    clips_all = lax.all_gather(clip_pair, "cx", axis=0)
     key_hot = (clips_all[:, None, :] == clip_ids[0][None, :, None]).astype(jnp.bfloat16)
     attended = flash_attention(qvis, queries, kv_all, key_hot, score_scale)
+    tok = clip_of.shape[0]
+    att_back = lax.ppermute(attended[tok:], "core", swap)
     ow = out_weight.reshape(heads_here * head_size, out_weight.shape[2])
-    mixed = jnp.dot(attended, ow, preferred_element_type=jnp.float32).astype(jnp.bfloat16)
+    ow_mine = lax.dynamic_slice_in_dim(ow, core * half * head_size, half * head_size, axis=0)
+    ow_other = lax.dynamic_slice_in_dim(ow, (1 - core) * half * head_size, half * head_size, axis=0)
+    mixed = (
+        jnp.dot(attended[:tok], ow_mine, preferred_element_type=jnp.float32)
+        + jnp.dot(att_back, ow_other, preferred_element_type=jnp.float32)
+    ).astype(jnp.bfloat16)
     groups = lax.axis_size("head")
     parts = mixed.reshape(groups, mixed.shape[0] // groups, mixed.shape[1])
     parts = lax.all_to_all(parts, "head", 0, 0)
@@ -111,15 +127,17 @@
 
 
 def solution(mesh):
+    ctx = mesh.shape["ctx"]
+    fine = Mesh(mesh.devices.reshape(ctx // 2, 2, mesh.shape["head"]), ("cx", "core", "head"))
     placed = (
-        P("ctx", None),
+        P(("cx", "core"), None),
         P(None, None, "head", None),
         P("head", None, None),
         P(),
         P(),
-        P("ctx"),
+        P(("cx", "core")),
         P(),
     )
     return jax.shard_map(
-        per_device, mesh=mesh, in_specs=placed, out_specs=P(("ctx", "head"), None), check_vma=False
+        per_device, mesh=fine, in_specs=placed, out_specs=P(("cx", "core", "head"), None), check_vma=False
     )

time: 243 us -> 248 us (1.021)
  blocking collectives: 75.4 us -> 86.9 us
  waiting for transfers between devices: 86 us -> 75.2 us
    all_gather x1, waiting for transfers between devices: 86 us -> 71.9 us  [per_device(): kv_all = lax.all_gather(kv_local, 'cx', axis=0)]
    all_gather x1, blocking collectives: 21.2 us -> 32.5 us  [per_device(): clips_all = lax.all_gather(clip_pair, 'cx', axis=0)]
    ppermute x0 -> x3, waiting for transfers between devices: none -> 3.3 us  [the longest x1 2.27 us: per_device(): recv = lax.ppermute(other, 'core', swap)]
  transfers between devices with their start and end apart: 1 -> 4, of which waited for: 1 -> 3; matrix products, arithmetic and copies ran while one was open for 1% -> 3% of each run, Pallas kernels for 0% -> 0%
where the time goes in v4:
time: 248 us; the launch traced here: 246 us
  blocking collectives  86.9 us (35%)
  waiting for transfers between devices  75.2 us (30%)
  Pallas kernels  38.8 us (16%)
  matrix products  20.6 us (8%)
  between operations  13.5 us (5%)
  other arithmetic  7.84 us (3%)
    all_gather x1, waiting for transfers between devices, per_device(): kv_all = lax.all_gather(kv_local, 'cx', axis=0)  71.9 us
    all_to_all x1, blocking collectives, per_device(): parts = lax.all_to_all(parts, 'head', 0, 0)  54.4 us
    pallas_call x1, Pallas kernels, flash_attention(): pl.pallas_call(kernel, grid=(nsteps,), in_specs=[pl.BlockSpec((nq, clip_c...  38.8 us
    all_gather x1, blocking collectives, per_device(): clips_all = lax.all_gather(clip_pair, 'cx', axis=0)  32.5 us
    dot_general x1, matrix products, per_device(): jnp.einsum('td,dchk->chtk', moduled, qkv_weight, preferred_element_type=j...  10.1 us
    dot_general x1, matrix products, per_device(): modulation = jnp.dot(level_hot, mod_table, precision=lax.Precision.HIGHEST)  5.58 us
  transfers between devices with their start and end apart: 4, of which 3 were waited for; matrix products, arithmetic and copies ran while one was open for 3% of the time, Pallas kernels for 0%

profile of v4, /device:TPU:6, one launch (start us, length us, event | category | flops | bytes accessed | tf_op | source)
XLA Modules:
  0.0 245.6 jit_solution(13888928071187986999)
XLA Ops:
  6.5 0.8 select_reduce_fusion
  7.4 0.1 copy-done
  7.5 5.6 %fusion.2 = bf16[512,4096,1,1]{1,0,3,2:T(8,128)(2,1)S(1)} fusion(f32[16,4096]{1,0:T(8,128)S(1)} %copy-done, bf16[512,4096]{1,0:T(8,128)(2,1)} %param.7, s32[512]{0:T(512)S(1)} %select_reduce_fusion), kind=kOutput, calls=%fused_computation.4 | convolution fusion | flops 411049984 | bytes 8652800 | tf_op jit(solution)/shard_map/dot_general | solution.py:91
  13.1 10.1 %fusion.7 = bf16[512,3,4,128]{3,0,2,1:T(8,128)(2,1)S(1)} fusion(bf16[512,4096,1,1]{1,0,3,2:T(8,128)(2,1)S(1)} %fusion.2, bf16[4096,3,4,128]{3,2,1,0:T(4,128)(2,1)} %param.8), kind=kOutput, calls=%fused_computation.10 | convolution fusion | flops 6443237376 | bytes 18350080 | tf_op jit(solution)/shard_map/td,dchk->chtk/dot_general | solution.py:93
  23.2 0.1 dynamic-slice_bitcast_fusion.1
  23.3 0.1 collective-permute-start.1
  23.4 2.3 collective-permute-done.1
  25.7 1.0 pad_maximum_fusion
  26.7 0.0 all-gather.4.cloned.1.call-update
  26.8 0.2 collective-permute-start
  27.0 1.0 collective-permute-done
  28.0 32.5 %all-gather.1 = s32[8192]{0:T(1024)S(1)} all-gather(s32[1024]{0:T(1024)S(1)} %constant_dynamic-update-slice_fusion), channel_id=3, replica_groups=mesh['cx'=8,'core'=2,'head'=8] {'cx'}, dimensions={0}, use_global_device_ids=true | all-gather | bytes 36864 | tf_op jit(solution)/shard_map/all_gather | solution.py:111
  60.6 0.6 convolution_convert_fusion
  61.2 0.8 copy.15.qvis_ref
  62.0 1.3 fusion.6.kh_ref
  63.3 0.8 maximum_bitcast_fusion.q_ref
  64.1 71.9 %all-gather.4.cloned.1.call-done = bf16[16,2,1024,128]{3,2,1,0:T(8,128)(2,1)} async-done(((bf16[2,2,1024,128]{3,2,1,0:T(8,128)(2,1)}), bf16[16,2,1024,128]{3,2,1,0:T(8,128)(2,1)}) %all-gather.4.cloned.1.call-update) | async-done | bytes 8388624 | tf_op jit(solution)/shard_map/all_gather | solution.py:110
  136.1 38.8 %shard_map.73 = bf16[1024,256]{1,0:T(8,128)(2,1)} custom-call(bf16[1024,64]{1,0:T(8,128)(2,1)} %copy.15.qvis_ref, bf16[2,1024,128]{2,1,0:T(8,128)(2,1)} %maximum_bitcast_fusion.q_ref, bf16[8,2,2,1024,128]{4,3,2,1,0:T(8,128)(2,1)} %bitcast.19, bf16[8,64,1024]{2,1,0:T(8,128)(2,1)} %fusion.6.kh_ref), custom_call_target="tpu_custom_call" | custom-call | flops 9663676416 | bytes 9437184 | tf_op jit(solution)/shard_map/pallas_call | solution.py:60
  174.9 1.0 slice.17
  175.8 0.3 collective-permute-start.2
  176.1 3.1 %fusion.4 = f32[512,4096]{1,0:T(8,128)S(1)} fusion(bf16[512,4096]{1,0:T(8,128)(2,1)} %bitcast.17, s32[]{:T(128)S(6)} %select_n.19, bf16[1024,256]{1,0:T(8,128)(2,1)} %shard_map.73), kind=kOutput, calls=%fused_computation.6 | convolution fusion | flops 1073741824 | bytes 10747908 | tf_op jit(solution)/shard_map/dot_general | solution.py:120
  179.2 1.3 add_convert_fusion
  180.5 54.4 %all_to_all.5 = bf16[8,64,4096]{2,1,0:T(8,128)(2,1)} all-to-all(bf16[8,64,4096]{2,1,0:T(8,128)(2,1)S(1)} %bitcast.16), channel_id=1, replica_groups=mesh['cx'=8,'core'=2,'head'=8] {'head'}, dimensions={0} | all-to-all | bytes 8388608 | tf_op jit(solution)/shard_map/all_to_all | solution.py:125
  234.9 3.8 %reduce_sum.22 = bf16[64,4096]{1,0:T(8,128)(2,1)} reduce(bf16[8,64,4096]{2,1,0:T(8,128)(2,1)} %all_to_all.5, bf16[]{:T(256)} %constant.24.clone.1), dimensions={0}, to_apply=%region_1.2 | reduce | flops 1835008 | bytes 4718594 | tf_op jit(solution)/shard_map/reduce_sum | solution.py:126
  (13 shorter events, 0.0 us)
Async XLA Ops:
  6.5 1.0 copy-start
  6.5 129.5 %all-gather.4.cloned.1.call-start = ((), (), s32[]{:S(2)}) async-start(), calls=%async_computation.1 | async-start | bytes 9437184 | tf_op jit(solution)/shard_map/all_gather | solution.py:110
  23.2 3.6 %copy-start.2 = (s32[512]{0:T(512)S(1)}, s32[512]{0:T(512)}, u32[]{:S(2)}) copy-start(s32[512]{0:T(512)} %param.12) | copy-start | bytes 6148
  23.2 37.4 %copy-start.3 = (s32[64,64]{1,0:T(8,128)S(1)}, s32[64,64]{1,0:T(8,128)}, u32[]{:S(2)}) copy-start(s32[64,64]{1,0:T(8,128)} %param.13) | copy-start | bytes 49156
  23.3 2.4 collective-permute-start.1
  26.8 1.2 collective-permute-start
  175.8 3.4 %collective-permute-start.2 = (bf16[512,256]{1,0:T(8,128)(2,1)S(1)}, bf16[512,256]{1,0:T(8,128)(2,1)S(1)}, u32[]{:S(2)}, u32[]{:S(2)}) collective-permute-start(bf16[512,256]{1,0:T(8,128)(2,1)S(1)} %slice.17), channel_id=1, source_target_pairs={{0,8},{8,0},{1,9},{9,1},{2,10},{10,2},{3,11},{11,3},{4,12},{12,4},... | collective-permute-start | bytes 786440 | tf_op jit(solution)/shard_map/ppermute | solution.py:115
  176.1 3.1 %copy-start.1 = (bf16[4,128,4096]{2,1,0:T(8,128)(2,1)S(1)}, bf16[4,128,4096]{2,1,0:T(8,128)(2,1)}, u32[]{:S(2)}) copy-start(bf16[4,128,4096]{2,1,0:T(8,128)(2,1)} %param.9) | copy-start | bytes 12582916
Sparse Core Ops, SparseCore 0:
  26.9 109.1 all-gather.3

commit v5 on v3

--- a/solution.py
+++ b/solution.py
@@ -7,7 +7,7 @@
 from jax import lax
 from jax.experimental import pallas as pl
 from jax.experimental.pallas import tpu as pltpu
-from jax.sharding import PartitionSpec as P
+from jax.sharding import Mesh, PartitionSpec as P
 
 
 def attn_kernel(qvis_ref, q_ref, kv_ref, kh_ref, o_ref, m_sc, l_sc, acc_sc, *, scale, nsteps, heads):
@@ -78,11 +78,77 @@
     )(qvis, q, kv_all, key_hot)
 
 
+def attn_kernel1(qvis_ref, q_ref, k_ref, v_ref, kh_ref, o_ref, m_sc, l_sc, acc_sc, *, scale, nsteps):
+    j = pl.program_id(0)
+    lanes = m_sc.shape[1]
+
+    @pl.when(j == 0)
+    def _():
+        m_sc[...] = jnp.full(m_sc.shape, -1e30, jnp.float32)
+        l_sc[...] = jnp.zeros(l_sc.shape, jnp.float32)
+        acc_sc[...] = jnp.zeros(acc_sc.shape, jnp.float32)
+
+    allowed = jnp.dot(qvis_ref[...], kh_ref[...], preferred_element_type=jnp.float32)
+    bias = jnp.where(allowed > 0.5, 0.0, -jnp.inf).astype(jnp.float32)
+    bk = bias.shape[1]
+    s = lax.dot_general(q_ref[...], k_ref[...], (((1,), (1,)), ((), ())), preferred_element_type=jnp.float32)
+    s = s * scale + bias
+    m_old = m_sc[...]
+    m_new = jnp.maximum(m_old, jnp.max(s, axis=1, keepdims=True))
+    p = jnp.exp(s - jnp.tile(m_new, (1, bk // lanes)))
+    alpha = jnp.exp(m_old - m_new)
+    l_sc[...] = l_sc[...] * alpha + jnp.sum(p, axis=1, keepdims=True)
+    acc_sc[...] = acc_sc[...] * alpha + jnp.dot(
+        p.astype(jnp.bfloat16), v_ref[...], preferred_element_type=jnp.float32
+    )
+    m_sc[...] = m_new
+
+    @pl.when(j == nsteps - 1)
+    def _():
+        o_ref[...] = (acc_sc[...] / l_sc[...]).astype(o_ref.dtype)
+
+
+def flash_attention1(qvis, q, kv_all, key_hot, scale, tok):
+    nq, hd = q.shape
+    sources = kv_all.shape[0]
+    clip_count = qvis.shape[1]
+    bk = math.gcd(tok, 512)
+    sub = tok // bk
+    nsteps = sources * sub
+    kernel = functools.partial(attn_kernel1, scale=scale, nsteps=nsteps)
+    cost = pl.CostEstimate(
+        flops=4 * nq * sources * tok * hd + 2 * nq * clip_count * sources * tok,
+        transcendentals=nq * sources * tok,
+        bytes_accessed=kv_all.size * 2 + q.size * 4,
+    )
+    return pl.pallas_call(
+        kernel,
+        grid=(nsteps,),
+        in_specs=[
+            pl.BlockSpec((nq, clip_count), lambda j: (0, 0)),
+            pl.BlockSpec((nq, hd), lambda j: (0, 0)),
+            pl.BlockSpec((None, bk, hd), lambda j: (j // sub, j % sub, 0)),
+            pl.BlockSpec((None, bk, hd), lambda j: (j // sub, sub + j % sub, 0)),
+            pl.BlockSpec((None, clip_count, bk), lambda j: (j // sub, 0, j % sub)),
+        ],
+        out_specs=pl.BlockSpec((nq, hd), lambda j: (0, 0)),
+        out_shape=jax.ShapeDtypeStruct((nq, hd), jnp.bfloat16),
+        scratch_shapes=[
+            pltpu.VMEM((nq, 128), jnp.float32),
+            pltpu.VMEM((nq, 128), jnp.float32),
+            pltpu.VMEM((nq, hd), jnp.float32),
+        ],
+        compiler_params=pltpu.CompilerParams(dimension_semantics=("arbitrary",)),
+        cost_estimate=cost,
+    )(qvis, q, kv_all, kv_all, key_hot)
+
+
 def per_device(activations, qkv_weight, out_weight, mod_table, clip_level, clip_of, visible):
     heads_here = qkv_weight.shape[2]
     head_size = qkv_weight.shape[3]
     clip_count = visible.shape[0]
     level_count = mod_table.shape[0]
+    tok = clip_of.shape[0]
     clip_ids = lax.broadcasted_iota(jnp.int32, (1, clip_count), 1)
     level_ids = lax.broadcasted_iota(jnp.int32, (1, level_count), 1)
     tok_hot = clip_of[:, None] == clip_ids
@@ -91,19 +157,40 @@
     modulation = jnp.dot(level_hot, mod_table, precision=lax.Precision.HIGHEST)
     moduled = (activations.astype(jnp.float32) * (1.0 + modulation)).astype(jnp.bfloat16)
     qkv = jnp.einsum(
-        "td,dchk->chtk", moduled, qkv_weight, preferred_element_type=jnp.float32
+        "td,dchk->hctk", moduled, qkv_weight, preferred_element_type=jnp.float32
     ).astype(jnp.bfloat16)
-    queries = qkv[0]
-    kv_local = qkv[1:3]
-    query_hot = tok_hot.astype(jnp.float32)
+    lane = head_size
+    clip_rows = tok // lane
+    pad_rows = -clip_rows % 8
+    clip_slab = jnp.concatenate(
+        [clip_of.astype(jnp.bfloat16).reshape(clip_rows, lane), jnp.zeros((pad_rows, lane), jnp.bfloat16)]
+    )
+    payload = jnp.concatenate(
+        [qkv.reshape(heads_here, 3 * tok, lane), jnp.broadcast_to(clip_slab, (heads_here,) + clip_slab.shape)],
+        axis=1,
+    )
+    exch = lax.all_to_all(payload, "yc", 0, 0, tiled=True)
+    group_tok = heads_here * tok
+    queries = exch[:, 0:tok].reshape(group_tok, lane)
+    keys = exch[:, tok:2 * tok].reshape(group_tok, lane)
+    values = exch[:, 2 * tok:3 * tok].reshape(group_tok, lane)
+    clip_group = exch[:, 3 * tok:3 * tok + clip_rows].reshape(group_tok)
+    group_rows = group_tok // lane
+    kv_pad = -group_rows % 8
+    kv_payload = jnp.concatenate(
+        [keys, values, clip_group.reshape(group_rows, lane), jnp.zeros((kv_pad, lane), jnp.bfloat16)]
+    )
+    kv_all = lax.all_gather(kv_payload, "x", axis=0)
+    key_clips = kv_all[:, 2 * group_tok:2 * group_tok + group_rows].reshape(kv_all.shape[0], group_tok)
+    key_hot = (key_clips.astype(jnp.int32)[:, None, :] == clip_ids[0][None, :, None]).astype(jnp.bfloat16)
+    query_hot = (clip_group.astype(jnp.int32)[:, None] == clip_ids).astype(jnp.float32)
     qvis = jnp.dot(query_hot, visible.astype(jnp.float32), precision=lax.Precision.HIGHEST).astype(jnp.bfloat16)
     score_scale = float(np.float32(1.0) / np.sqrt(np.float32(head_size)))
-    kv_all = lax.all_gather(kv_local, "ctx", axis=0)
-    clips_all = lax.all_gather(clip_of, "ctx", axis=0)
-    key_hot = (clips_all[:, None, :] == clip_ids[0][None, :, None]).astype(jnp.bfloat16)
-    attended = flash_attention(qvis, queries, kv_all, key_hot, score_scale)
-    ow = out_weight.reshape(heads_here * head_size, out_weight.shape[2])
-    mixed = jnp.dot(attended, ow, preferred_element_type=jnp.float32).astype(jnp.bfloat16)
+    attended = flash_attention1(qvis, queries, kv_all, key_hot, score_scale, group_tok)
+    back = lax.all_to_all(attended.reshape(heads_here, tok, lane), "yc", 0, 0, tiled=True)
+    mixed = jnp.einsum(
+        "hrd,hdo->ro", back, out_weight, preferred_element_type=jnp.float32
+    ).astype(jnp.bfloat16)
     groups = lax.axis_size("head")
     parts = mixed.reshape(groups, mixed.shape[0] // groups, mixed.shape[1])
     parts = lax.all_to_all(parts, "head", 0, 0)
@@ -111,15 +198,18 @@
 
 
 def solution(mesh):
+    ctx = mesh.shape["ctx"]
+    heads = 4
+    fine = Mesh(mesh.devices.reshape(ctx // heads, heads, mesh.shape["head"]), ("x", "yc", "head"))
     placed = (
-        P("ctx", None),
+        P(("x", "yc"), None),
         P(None, None, "head", None),
         P("head", None, None),
         P(),
         P(),
-        P("ctx"),
+        P(("x", "yc")),
         P(),
     )
     return jax.shard_map(
-        per_device, mesh=mesh, in_specs=placed, out_specs=P(("ctx", "head"), None), check_vma=False
-    )
+        per_device, mesh=fine, in_specs=placed, out_specs=P(("x", "yc", "head"), None), check_vma=False
+    )

time: 243 us -> 233 us (0.959)
  waiting for transfers between devices: 86 us -> 44.6 us
  blocking collectives: 75.4 us -> 94.2 us
  Pallas kernels: 36.8 us -> 46.4 us
  other arithmetic: 6.02 us -> 8.53 us
    all_gather x1, waiting for transfers between devices: 86 us -> 44.6 us  [per_device(): kv_all = lax.all_gather(kv_payload, 'x', axis=0)]
    all_to_all x0 -> x2, blocking collectives: none -> 40.7 us  [the longest x1 25.9 us: per_device(): exch = lax.all_to_all(payload, 'yc', 0, 0, tiled=True)]
    all_gather x1 -> x0, blocking collectives: 21.2 us -> none  [per_device(): clips_all = lax.all_gather(clip_of, 'ctx', axis=0)]
    pallas_call x1, Pallas kernels: 36.8 us -> 46.4 us  [flash_attention1(): pl.pallas_call(kernel, grid=(nsteps,), in_specs=[pl.BlockSpec((nq, clip_c...]
where the time goes in v5:
time: 233 us; the launch traced here: 231 us
  blocking collectives  94.2 us (40%)
  Pallas kernels  46.4 us (20%)
  waiting for transfers between devices  44.6 us (19%)
  matrix products  21.3 us (9%)
  between operations  13.5 us (6%)
  other arithmetic  8.53 us (4%)
    all_to_all x1, blocking collectives, per_device(): parts = lax.all_to_all(parts, 'head', 0, 0)  53.4 us
    pallas_call x1, Pallas kernels, flash_attention1(): pl.pallas_call(kernel, grid=(nsteps,), in_specs=[pl.BlockSpec((nq, clip_c...  46.4 us
    all_gather x1, waiting for transfers between devices, per_device(): kv_all = lax.all_gather(kv_payload, 'x', axis=0)  44.6 us
    all_to_all x1, blocking collectives, per_device(): exch = lax.all_to_all(payload, 'yc', 0, 0, tiled=True)  25.9 us
    all_to_all x1, blocking collectives, per_device(): lax.all_to_all(attended.reshape(heads_here, tok, lane), 'yc', 0, 0, tiled...  14.8 us
    dot_general x1, matrix products, per_device(): jnp.einsum('td,dchk->hctk', moduled, qkv_weight, preferred_element_type=j...  10 us
    dot_general x1, matrix products, per_device(): modulation = jnp.dot(level_hot, mod_table, precision=lax.Precision.HIGHEST)  5.59 us
    dot_general x1, matrix products, per_device(): jnp.einsum('hrd,hdo->ro', back, out_weight, preferred_element_type=jnp.fl...  4.73 us
  transfers between devices with their start and end apart: 1, of which 1 were waited for; matrix products, arithmetic and copies ran while one was open for 1% of the time, Pallas kernels for 0%

profile of v5, /device:TPU:6, one launch (start us, length us, event | category | flops | bytes accessed | tf_op | source)
XLA Modules:
  0.0 230.5 jit_solution(14028907643173611303)
XLA Ops:
  6.5 0.0 copy-start
  6.5 0.0 all-gather.3.cloned.1.call-start
  6.5 0.7 convert_bitcast_fusion.1
  7.3 0.8 select_reduce_fusion
  8.1 0.0 copy-done
  8.1 5.6 %fusion.2 = bf16[512,4096,1,1]{1,0,3,2:T(8,128)(2,1)S(1)} fusion(f32[16,4096]{1,0:T(8,128)S(1)} %copy-done, bf16[512,4096]{1,0:T(8,128)(2,1)} %param.7, s32[512]{0:T(512)S(1)} %select_reduce_fusion), kind=kOutput, calls=%fused_computation.4 | convolution fusion | flops 411049984 | bytes 8652800 | tf_op jit(solution)/shard_map/dot_general | solution.py:157
  13.7 10.0 %fusion.7 = bf16[4,3,512,128]{3,2,0,1:T(8,128)(2,1)S(1)} fusion(bf16[512,4096,1,1]{1,0,3,2:T(8,128)(2,1)S(1)} %fusion.2, bf16[4096,3,4,128]{3,2,1,0:T(4,128)(2,1)} %param.8), kind=kOutput, calls=%fused_computation.10 | convolution fusion | flops 6443237376 | bytes 18350080 | tf_op jit(solution)/shard_map/td,dchk->hctk/dot_general | solution.py:159
  23.7 0.1 copy.17
  23.9 0.1 pad_maximum_fusion
  24.0 0.0 copy-start.1
  24.0 25.9 %all_to_all.15 = bf16[4,1544,128]{2,1,0:T(8,128)(2,1)S(1)} all-to-all(bf16[4,1544,128]{2,1,0:T(8,128)(2,1)S(1)} %pad_maximum_fusion), channel_id=1, replica_groups=mesh['x'=4,'yc'=4,'head'=8] {'yc'}, dimensions={0} | all-to-all | bytes 3162112 | tf_op jit(solution)/shard_map/all_to_all | solution.py:172
  49.9 0.9 fusion.13
  50.8 1.1 pad_maximum_fusion.1
  51.9 0.0 all-gather.3.cloned.1.call-update
  51.9 0.9 convolution_convert_fusion
  52.8 1.0 copy.18.qvis_ref
  53.9 44.6 %all-gather.3.cloned.1.call-done = bf16[16448,128]{1,0:T(8,128)(2,1)} async-done(((bf16[4112,128]{1,0:T(8,128)(2,1)}), bf16[16448,128]{1,0:T(8,128)(2,1)}) %all-gather.3.cloned.1.call-update) | async-done | bytes 4210704 | tf_op jit(solution)/shard_map/all_gather | solution.py:183
  98.4 0.7 convert_bitcast_fusion
  99.2 1.2 fusion.3.kh_ref
  100.4 46.4 %shard_map.73 = bf16[2048,128]{1,0:T(8,128)(2,1)} custom-call(bf16[2048,64]{1,0:T(8,128)(2,1)} %copy.18.qvis_ref, bf16[2048,128]{1,0:T(8,128)(2,1)} %bitcast.34, bf16[4,4112,128]{2,1,0:T(8,128)(2,1)} %bitcast.39, bf16[4,4112,128]{2,1,0:T(8,128)(2,1)} %bitcast.40, bf16[4,64,2048]{2,1,0:T(8,128)(2,1)} %fusion.3.kh_ref), custom_call_target="tpu_custom_call" | custom-call | flops 10737418240 | bytes 5259264 | tf_op jit(solution)/shard_map/pallas_call | solution.py:124
  146.8 14.8 %all_to_all.16 = bf16[4,512,128]{2,1,0:T(8,128)(2,1)S(1)} all-to-all(bf16[4,512,128]{2,1,0:T(8,128)(2,1)} %bitcast.33), channel_id=1, replica_groups=mesh['x'=4,'yc'=4,'head'=8] {'yc'}, dimensions={0} | all-to-all | bytes 1048576 | tf_op jit(solution)/shard_map/all_to_all | solution.py:190
  161.7 4.7 %bitcast_convert_fusion = bf16[512,4096]{1,0:T(8,128)(2,1)S(1)} fusion(bf16[4,512,128]{2,1,0:T(8,128)(2,1)S(1)} %all_to_all.16, bf16[4,128,4096]{2,1,0:T(8,128)(2,1)} %param.9), kind=kOutput, calls=%fused_computation.2 | convolution fusion | flops 2149580800 | bytes 8912896 | tf_op jit(solution)/shard_map/hrd,hdo->ro/dot_general | solution.py:191
  166.4 53.4 %all_to_all.17 = bf16[8,64,4096]{2,1,0:T(8,128)(2,1)} all-to-all(bf16[8,64,4096]{2,1,0:T(8,128)(2,1)S(1)} %bitcast.30), channel_id=1, replica_groups=mesh['x'=4,'yc'=4,'head'=8] {'head'}, dimensions={0} | all-to-all | bytes 8388608 | tf_op jit(solution)/shard_map/all_to_all | solution.py:196
  219.8 3.8 %reduce_sum.22 = bf16[64,4096]{1,0:T(8,128)(2,1)} reduce(bf16[8,64,4096]{2,1,0:T(8,128)(2,1)} %all_to_all.17, bf16[]{:T(256)} %constant.2.clone.1), dimensions={0}, to_apply=%region_1.2 | reduce | flops 1835008 | bytes 4718594 | tf_op jit(solution)/shard_map/reduce_sum | solution.py:197
  (6 shorter events, 0.0 us)
Async XLA Ops:
  6.5 1.5 copy-start
  6.5 91.9 %all-gather.3.cloned.1.call-start = ((), (), s32[]{:S(2)}) async-start(), calls=%async_computation.3 | async-start | bytes 5263360 | tf_op jit(solution)/shard_map/all_gather | solution.py:183
  24.0 28.0 %copy-start.1 = (s32[64,64]{1,0:T(8,128)S(1)}, s32[64,64]{1,0:T(8,128)}, u32[]{:S(2)}) copy-start(s32[64,64]{1,0:T(8,128)} %param.13) | copy-start | bytes 49156
Sparse Core Ops, SparseCore 0:
  52.0 46.3 all-gather.2

commit v6 on v5

--- a/solution.py
+++ b/solution.py
@@ -78,7 +78,7 @@
     )(qvis, q, kv_all, key_hot)
 
 
-def attn_kernel1(qvis_ref, q_ref, k_ref, v_ref, kh_ref, o_ref, m_sc, l_sc, acc_sc, *, scale, nsteps):
+def attn_kernel1(need_ref, qvis_ref, q_ref, k_ref, v_ref, kh_ref, o_ref, m_sc, l_sc, acc_sc, *, scale, nsteps, chunk):
     j = pl.program_id(0)
     lanes = m_sc.shape[1]
 
@@ -88,59 +88,74 @@
         l_sc[...] = jnp.zeros(l_sc.shape, jnp.float32)
         acc_sc[...] = jnp.zeros(acc_sc.shape, jnp.float32)
 
-    allowed = jnp.dot(qvis_ref[...], kh_ref[...], preferred_element_type=jnp.float32)
-    bias = jnp.where(allowed > 0.5, 0.0, -jnp.inf).astype(jnp.float32)
-    bk = bias.shape[1]
-    s = lax.dot_general(q_ref[...], k_ref[...], (((1,), (1,)), ((), ())), preferred_element_type=jnp.float32)
-    s = s * scale + bias
-    m_old = m_sc[...]
-    m_new = jnp.maximum(m_old, jnp.max(s, axis=1, keepdims=True))
-    p = jnp.exp(s - jnp.tile(m_new, (1, bk // lanes)))
-    alpha = jnp.exp(m_old - m_new)
-    l_sc[...] = l_sc[...] * alpha + jnp.sum(p, axis=1, keepdims=True)
-    acc_sc[...] = acc_sc[...] * alpha + jnp.dot(
-        p.astype(jnp.bfloat16), v_ref[...], preferred_element_type=jnp.float32
-    )
-    m_sc[...] = m_new
+    for c in range(q_ref.shape[0] // chunk):
+        rows = pl.ds(c * chunk, chunk)
+
+        @pl.when(need_ref[c, j] > 0)
+        def _():
+            allowed = jnp.dot(qvis_ref[rows, :], kh_ref[...], preferred_element_type=jnp.float32)
+            bias = jnp.where(allowed > 0.5, 0.0, -jnp.inf).astype(jnp.float32)
+            bk = bias.shape[1]
+            s = lax.dot_general(
+                q_ref[rows, :], k_ref[...], (((1,), (1,)), ((), ())), preferred_element_type=jnp.float32
+            )
+            s = s * scale + bias
+            m_old = m_sc[rows, :]
+            m_new = jnp.maximum(m_old, jnp.max(s, axis=1, keepdims=True))
+            p = jnp.exp(s - jnp.tile(m_new, (1, bk // lanes)))
+            alpha = jnp.exp(m_old - m_new)
+            l_sc[rows, :] = l_sc[rows, :] * alpha + jnp.sum(p, axis=1, keepdims=True)
+            acc_sc[rows, :] = acc_sc[rows, :] * alpha + jnp.dot(
+                p.astype(jnp.bfloat16), v_ref[...], preferred_element_type=jnp.float32
+            )
+            m_sc[rows, :] = m_new
 
     @pl.when(j == nsteps - 1)
     def _():
         o_ref[...] = (acc_sc[...] / l_sc[...]).astype(o_ref.dtype)
 
 
-def flash_attention1(qvis, q, kv_all, key_hot, scale, tok):
+def flash_attention1(qvis, q, kv_all, key_hot, query_clips, key_clips, scale, tok):
     nq, hd = q.shape
     sources = kv_all.shape[0]
     clip_count = qvis.shape[1]
     bk = math.gcd(tok, 512)
+    chunk = math.gcd(nq, 512)
     sub = tok // bk
     nsteps = sources * sub
-    kernel = functools.partial(attn_kernel1, scale=scale, nsteps=nsteps)
+    key_low = jnp.min(key_clips.reshape(nsteps, bk), axis=1)
+    query_high = jnp.max(query_clips.reshape(nq // chunk, chunk), axis=1)
+    need = (key_low[None, :] <= query_high[:, None]).astype(jnp.int32)
+    kernel = functools.partial(attn_kernel1, scale=scale, nsteps=nsteps, chunk=chunk)
     cost = pl.CostEstimate(
         flops=4 * nq * sources * tok * hd + 2 * nq * clip_count * sources * tok,
         transcendentals=nq * sources * tok,
         bytes_accessed=kv_all.size * 2 + q.size * 4,
     )
-    return pl.pallas_call(
-        kernel,
+    grid_spec = pltpu.PrefetchScalarGridSpec(
+        num_scalar_prefetch=1,
         grid=(nsteps,),
         in_specs=[
-            pl.BlockSpec((nq, clip_count), lambda j: (0, 0)),
-            pl.BlockSpec((nq, hd), lambda j: (0, 0)),
-            pl.BlockSpec((None, bk, hd), lambda j: (j // sub, j % sub, 0)),
-            pl.BlockSpec((None, bk, hd), lambda j: (j // sub, sub + j % sub, 0)),
-            pl.BlockSpec((None, clip_count, bk), lambda j: (j // sub, 0, j % sub)),
-        ],
-        out_specs=pl.BlockSpec((nq, hd), lambda j: (0, 0)),
-        out_shape=jax.ShapeDtypeStruct((nq, hd), jnp.bfloat16),
+            pl.BlockSpec((nq, clip_count), lambda j, n: (0, 0)),
+            pl.BlockSpec((nq, hd), lambda j, n: (0, 0)),
+            pl.BlockSpec((None, bk, hd), lambda j, n: (j // sub, j % sub, 0)),
+            pl.BlockSpec((None, bk, hd), lambda j, n: (j // sub, sub + j % sub, 0)),
+            pl.BlockSpec((None, clip_count, bk), lambda j, n: (j // sub, 0, j % sub)),
+        ],
+        out_specs=pl.BlockSpec((nq, hd), lambda j, n: (0, 0)),
         scratch_shapes=[
             pltpu.VMEM((nq, 128), jnp.float32),
             pltpu.VMEM((nq, 128), jnp.float32),
             pltpu.VMEM((nq, hd), jnp.float32),
         ],
+    )
+    return pl.pallas_call(
+        kernel,
+        grid_spec=grid_spec,
+        out_shape=jax.ShapeDtypeStruct((nq, hd), jnp.bfloat16),
         compiler_params=pltpu.CompilerParams(dimension_semantics=("arbitrary",)),
         cost_estimate=cost,
-    )(qvis, q, kv_all, kv_all, key_hot)
+    )(need, qvis, q, kv_all, kv_all, key_hot)
 
 
 def per_device(activations, qkv_weight, out_weight, mod_table, clip_level, clip_of, visible):
@@ -186,7 +201,9 @@
     query_hot = (clip_group.astype(jnp.int32)[:, None] == clip_ids).astype(jnp.float32)
     qvis = jnp.dot(query_hot, visible.astype(jnp.float32), precision=lax.Precision.HIGHEST).astype(jnp.bfloat16)
     score_scale = float(np.float32(1.0) / np.sqrt(np.float32(head_size)))
-    attended = flash_attention1(qvis, queries, kv_all, key_hot, score_scale, group_tok)
+    attended = flash_attention1(
+        qvis, queries, kv_all, key_hot, clip_group.astype(jnp.int32), key_clips.astype(jnp.int32), score_scale, group_tok
+    )
     back = lax.all_to_all(attended.reshape(heads_here, tok, lane), "yc", 0, 0, tiled=True)
     mixed = jnp.einsum(
         "hrd,hdo->ro", back, out_weight, preferred_element_type=jnp.float32

time: 233 us -> 236 us (1.013)
  Pallas kernels: 46.4 us -> 49.7 us
    pallas_call x1, Pallas kernels: 46.4 us -> 49.7 us  [flash_attention1(): pl.pallas_call(kernel, grid_spec=grid_spec, out_shape=jax.ShapeDtypeStruc...]
where the time goes in v6:
time: 236 us; the launch traced here: 235 us
  blocking collectives  94.1 us (40%)
  Pallas kernels  49.7 us (21%)
  waiting for transfers between devices  44.4 us (19%)
  matrix products  21.3 us (9%)
  between operations  13.5 us (6%)
  other arithmetic  10.3 us (4%)
    all_to_all x1, blocking collectives, per_device(): parts = lax.all_to_all(parts, 'head', 0, 0)  53.4 us
    pallas_call x1, Pallas kernels, flash_attention1(): pl.pallas_call(kernel, grid_spec=grid_spec, out_shape=jax.ShapeDtypeStruc...  49.7 us
    all_gather x1, waiting for transfers between devices, per_device(): kv_all = lax.all_gather(kv_payload, 'x', axis=0)  44.4 us
    all_to_all x1, blocking collectives, per_device(): exch = lax.all_to_all(payload, 'yc', 0, 0, tiled=True)  25.9 us
    all_to_all x1, blocking collectives, per_device(): lax.all_to_all(attended.reshape(heads_here, tok, lane), 'yc', 0, 0, tiled...  14.8 us
    dot_general x1, matrix products, per_device(): jnp.einsum('td,dchk->hctk', moduled, qkv_weight, preferred_element_type=j...  10 us
    dot_general x1, matrix products, per_device(): modulation = jnp.dot(level_hot, mod_table, precision=lax.Precision.HIGHEST)  5.59 us
    dot_general x1, matrix products, per_device(): jnp.einsum('hrd,hdo->ro', back, out_weight, preferred_element_type=jnp.fl...  4.73 us
  transfers between devices with their start and end apart: 1, of which 1 were waited for; matrix products, arithmetic and copies ran while one was open for 1% of the time, Pallas kernels for 0%

profile of v6, /device:TPU:6, one launch (start us, length us, event | category | flops | bytes accessed | tf_op | source)
XLA Modules:
  0.0 235.5 jit_solution(627643892741756973)
XLA Ops:
  6.5 0.7 convert_bitcast_fusion.1
  7.3 0.8 select_reduce_fusion
  8.1 5.6 %fusion.2 = bf16[512,4096,1,1]{1,0,3,2:T(8,128)(2,1)S(1)} fusion(f32[16,4096]{1,0:T(8,128)S(1)} %copy-done, bf16[512,4096]{1,0:T(8,128)(2,1)} %param.7, s32[512]{0:T(512)S(1)} %select_reduce_fusion), kind=kOutput, calls=%fused_computation.4 | convolution fusion | flops 411049984 | bytes 8652800 | tf_op jit(solution)/shard_map/dot_general | solution.py:172
  13.7 10.0 %fusion.7 = bf16[4,3,512,128]{3,2,0,1:T(8,128)(2,1)S(1)} fusion(bf16[512,4096,1,1]{1,0,3,2:T(8,128)(2,1)S(1)} %fusion.2, bf16[4096,3,4,128]{3,2,1,0:T(4,128)(2,1)} %param.8), kind=kOutput, calls=%fused_computation.10 | convolution fusion | flops 6443237376 | bytes 18350080 | tf_op jit(solution)/shard_map/td,dchk->hctk/dot_general | solution.py:174
  23.7 0.1 copy.17
  23.9 0.1 pad_maximum_fusion
  24.0 25.9 %all_to_all.15 = bf16[4,1544,128]{2,1,0:T(8,128)(2,1)S(1)} all-to-all(bf16[4,1544,128]{2,1,0:T(8,128)(2,1)S(1)} %pad_maximum_fusion), channel_id=1, replica_groups=mesh['x'=4,'yc'=4,'head'=8] {'yc'}, dimensions={0} | all-to-all | bytes 3162112 | tf_op jit(solution)/shard_map/all_to_all | solution.py:187
  49.9 0.9 fusion.13
  50.8 1.1 pad_maximum_fusion.1
  51.9 0.9 convolution_convert_fusion
  52.8 1.0 copy.18.qvis_ref
  53.9 0.2 convert_reduce_fusion.1
  54.0 44.4 %all-gather.3.cloned.1.call-done = bf16[16448,128]{1,0:T(8,128)(2,1)} async-done(((bf16[4112,128]{1,0:T(8,128)(2,1)}), bf16[16448,128]{1,0:T(8,128)(2,1)}) %all-gather.3.cloned.1.call-update) | async-done | bytes 4210704 | tf_op jit(solution)/shard_map/all_gather | solution.py:198
  98.4 0.9 convert_reduce_fusion
  99.3 0.7 convert_bitcast_fusion
  100.0 0.1 reduce_min.14
  100.1 1.2 fusion.3.kh_ref
  101.3 0.1 reduce_min.18
  101.5 0.7 compare_convert_fusion.need_ref
  102.1 49.7 %shard_map.73 = bf16[2048,128]{1,0:T(8,128)(2,1)} custom-call(s32[4,16]{1,0:T(4,128)} %compare_convert_fusion.need_ref, bf16[2048,64]{1,0:T(8,128)(2,1)} %copy.18.qvis_ref, bf16[2048,128]{1,0:T(8,128)(2,1)} %bitcast.33, bf16[4,4112,128]{2,1,0:T(8,128)(2,1)} %bitcast.39, bf16[4,4112,128]{2,1,0:T(8,128)(2,1)} %bitcast.40, bf16[4,64,2048]{2,1,0:T(8,128)(2,1)} %fusion.3.kh_ref), custom_call_target="tpu_custom_call" | custom-call | flops 10737418240 | bytes 5259264 | tf_op jit(solution)/shard_map/pallas_call | solution.py:152
  151.8 14.8 %all_to_all.16 = bf16[4,512,128]{2,1,0:T(8,128)(2,1)S(1)} all-to-all(bf16[4,512,128]{2,1,0:T(8,128)(2,1)} %bitcast.32), channel_id=1, replica_groups=mesh['x'=4,'yc'=4,'head'=8] {'yc'}, dimensions={0} | all-to-all | bytes 1048576 | tf_op jit(solution)/shard_map/all_to_all | solution.py:207
  166.7 4.7 %bitcast_convert_fusion = bf16[512,4096]{1,0:T(8,128)(2,1)S(1)} fusion(bf16[4,512,128]{2,1,0:T(8,128)(2,1)S(1)} %all_to_all.16, bf16[4,128,4096]{2,1,0:T(8,128)(2,1)} %param.9), kind=kOutput, calls=%fused_computation.2 | convolution fusion | flops 2149580800 | bytes 8912896 | tf_op jit(solution)/shard_map/hrd,hdo->ro/dot_general | solution.py:208
  171.4 53.4 %all_to_all.17 = bf16[8,64,4096]{2,1,0:T(8,128)(2,1)} all-to-all(bf16[8,64,4096]{2,1,0:T(8,128)(2,1)S(1)} %bitcast.29), channel_id=1, replica_groups=mesh['x'=4,'yc'=4,'head'=8] {'head'}, dimensions={0} | all-to-all | bytes 8388608 | tf_op jit(solution)/shard_map/all_to_all | solution.py:213
  224.8 3.8 %reduce_sum.22 = bf16[64,4096]{1,0:T(8,128)(2,1)} reduce(bf16[8,64,4096]{2,1,0:T(8,128)(2,1)} %all_to_all.17, bf16[]{:T(256)} %constant.2.clone.1), dimensions={0}, to_apply=%region_4.5 | reduce | flops 1835008 | bytes 4718594 | tf_op jit(solution)/shard_map/reduce_sum | solution.py:214
  (10 shorter events, 0.1 us)
Async XLA Ops:
  6.5 1.5 copy-start
  6.5 91.9 %all-gather.3.cloned.1.call-start = ((), (), s32[]{:S(2)}) async-start(), calls=%async_computation.3 | async-start | bytes 5263360 | tf_op jit(solution)/shard_map/all_gather | solution.py:198
  24.0 28.0 %copy-start.1 = (s32[64,64]{1,0:T(8,128)S(1)}, s32[64,64]{1,0:T(8,128)}, u32[]{:S(2)}) copy-start(s32[64,64]{1,0:T(8,128)} %param.13) | copy-start | bytes 49156
Sparse Core Ops, SparseCore 0:
  52.0 46.3 all-gather.2

commit v7 on v5

--- a/solution.py
+++ b/solution.py
@@ -78,16 +78,8 @@
     )(qvis, q, kv_all, key_hot)
 
 
-def attn_kernel1(qvis_ref, q_ref, k_ref, v_ref, kh_ref, o_ref, m_sc, l_sc, acc_sc, *, scale, nsteps):
-    j = pl.program_id(0)
+def attn_body(qvis_ref, q_ref, k_ref, v_ref, kh_ref, m_sc, l_sc, acc_sc, scale):
     lanes = m_sc.shape[1]
-
-    @pl.when(j == 0)
-    def _():
-        m_sc[...] = jnp.full(m_sc.shape, -1e30, jnp.float32)
-        l_sc[...] = jnp.zeros(l_sc.shape, jnp.float32)
-        acc_sc[...] = jnp.zeros(acc_sc.shape, jnp.float32)
-
     allowed = jnp.dot(qvis_ref[...], kh_ref[...], preferred_element_type=jnp.float32)
     bias = jnp.where(allowed > 0.5, 0.0, -jnp.inf).astype(jnp.float32)
     bk = bias.shape[1]
@@ -103,44 +95,110 @@
     )
     m_sc[...] = m_new
 
+
+def local_kernel(qvis_ref, q_ref, k_ref, v_ref, kh_ref, m_ref, l_ref, acc_ref, *, scale):
+    j = pl.program_id(0)
+
+    @pl.when(j == 0)
+    def _():
+        m_ref[...] = jnp.full(m_ref.shape, -1e30, jnp.float32)
+        l_ref[...] = jnp.zeros(l_ref.shape, jnp.float32)
+        acc_ref[...] = jnp.zeros(acc_ref.shape, jnp.float32)
+
+    attn_body(qvis_ref, q_ref, k_ref, v_ref, kh_ref, m_ref, l_ref, acc_ref, scale)
+
+
+def remote_kernel(own_ref, qvis_ref, q_ref, k_ref, v_ref, kh_ref, m_in, l_in, acc_in, o_ref, m_sc, l_sc, acc_sc, *, scale, nsteps):
+    j = pl.program_id(0)
+
+    @pl.when(j == 0)
+    def _():
+        m_sc[...] = m_in[...]
+        l_sc[...] = l_in[...]
+        acc_sc[...] = acc_in[...]
+
+    attn_body(qvis_ref, q_ref, k_ref, v_ref, kh_ref, m_sc, l_sc, acc_sc, scale)
+
     @pl.when(j == nsteps - 1)
     def _():
         o_ref[...] = (acc_sc[...] / l_sc[...]).astype(o_ref.dtype)
 
 
-def flash_attention1(qvis, q, kv_all, key_hot, scale, tok):
+def attend_local(qvis, q, keys, values, key_hot, scale):
+    nq, hd = q.shape
+    tok = keys.shape[0]
+    clip_count = qvis.shape[1]
+    bk = math.gcd(tok, 512)
+    nsteps = tok // bk
+    state = jax.ShapeDtypeStruct((nq, 128), jnp.float32)
+    return pl.pallas_call(
+        functools.partial(local_kernel, scale=scale),
+        grid=(nsteps,),
+        in_specs=[
+            pl.BlockSpec((nq, clip_count), lambda j: (0, 0)),
+            pl.BlockSpec((nq, hd), lambda j: (0, 0)),
+            pl.BlockSpec((bk, hd), lambda j: (j, 0)),
+            pl.BlockSpec((bk, hd), lambda j: (j, 0)),
+            pl.BlockSpec((clip_count, bk), lambda j: (0, j)),
+        ],
+        out_specs=[
+            pl.BlockSpec((nq, 128), lambda j: (0, 0)),
+            pl.BlockSpec((nq, 128), lambda j: (0, 0)),
+            pl.BlockSpec((nq, hd), lambda j: (0, 0)),
+        ],
+        out_shape=[state, state, jax.ShapeDtypeStruct((nq, hd), jnp.float32)],
+        compiler_params=pltpu.CompilerParams(dimension_semantics=("arbitrary",)),
+        cost_estimate=pl.CostEstimate(
+            flops=4 * nq * tok * hd + 2 * nq * clip_count * tok,
+            transcendentals=nq * tok,
+            bytes_accessed=4 * tok * hd + 3 * nq * 512,
+        ),
+    )(qvis, q, keys, values, key_hot)
+
+
+def attend_remote(own, qvis, q, kv_all, key_hot, carry, scale, tok):
     nq, hd = q.shape
     sources = kv_all.shape[0]
     clip_count = qvis.shape[1]
     bk = math.gcd(tok, 512)
     sub = tok // bk
-    nsteps = sources * sub
-    kernel = functools.partial(attn_kernel1, scale=scale, nsteps=nsteps)
-    cost = pl.CostEstimate(
-        flops=4 * nq * sources * tok * hd + 2 * nq * clip_count * sources * tok,
-        transcendentals=nq * sources * tok,
-        bytes_accessed=kv_all.size * 2 + q.size * 4,
-    )
-    return pl.pallas_call(
-        kernel,
+    nsteps = (sources - 1) * sub
+
+    def src(j, o):
+        return (o[0] + 1 + j // sub) % sources
+
+    kernel = functools.partial(remote_kernel, scale=scale, nsteps=nsteps)
+    grid_spec = pltpu.PrefetchScalarGridSpec(
+        num_scalar_prefetch=1,
         grid=(nsteps,),
         in_specs=[
-            pl.BlockSpec((nq, clip_count), lambda j: (0, 0)),
-            pl.BlockSpec((nq, hd), lambda j: (0, 0)),
-            pl.BlockSpec((None, bk, hd), lambda j: (j // sub, j % sub, 0)),
-            pl.BlockSpec((None, bk, hd), lambda j: (j // sub, sub + j % sub, 0)),
-            pl.BlockSpec((None, clip_count, bk), lambda j: (j // sub, 0, j % sub)),
-        ],
-        out_specs=pl.BlockSpec((nq, hd), lambda j: (0, 0)),
-        out_shape=jax.ShapeDtypeStruct((nq, hd), jnp.bfloat16),
+            pl.BlockSpec((nq, clip_count), lambda j, o: (0, 0)),
+            pl.BlockSpec((nq, hd), lambda j, o: (0, 0)),
+            pl.BlockSpec((None, bk, hd), lambda j, o: (src(j, o), j % sub, 0)),
+            pl.BlockSpec((None, bk, hd), lambda j, o: (src(j, o), sub + j % sub, 0)),
+            pl.BlockSpec((None, clip_count, bk), lambda j, o: (src(j, o), 0, j % sub)),
+            pl.BlockSpec((nq, 128), lambda j, o: (0, 0)),
+            pl.BlockSpec((nq, 128), lambda j, o: (0, 0)),
+            pl.BlockSpec((nq, hd), lambda j, o: (0, 0)),
+        ],
+        out_specs=pl.BlockSpec((nq, hd), lambda j, o: (0, 0)),
         scratch_shapes=[
             pltpu.VMEM((nq, 128), jnp.float32),
             pltpu.VMEM((nq, 128), jnp.float32),
             pltpu.VMEM((nq, hd), jnp.float32),
         ],
+    )
+    return pl.pallas_call(
+        kernel,
+        grid_spec=grid_spec,
+        out_shape=jax.ShapeDtypeStruct((nq, hd), jnp.bfloat16),
         compiler_params=pltpu.CompilerParams(dimension_semantics=("arbitrary",)),
-        cost_estimate=cost,
-    )(qvis, q, kv_all, kv_all, key_hot)
+        cost_estimate=pl.CostEstimate(
+            flops=4 * nq * (sources - 1) * tok * hd + 2 * nq * clip_count * (sources - 1) * tok,
+            transcendentals=nq * (sources - 1) * tok,
+            bytes_accessed=kv_all.size * 2 + 3 * nq * 512,
+        ),
+    )(own, qvis, q, kv_all, kv_all, key_hot, *carry)
 
 
 def per_device(activations, qkv_weight, out_weight, mod_table, clip_level, clip_of, visible):
@@ -180,13 +238,16 @@
     kv_payload = jnp.concatenate(
         [keys, values, clip_group.reshape(group_rows, lane), jnp.zeros((kv_pad, lane), jnp.bfloat16)]
     )
+    query_hot = (clip_group.astype(jnp.int32)[:, None] == clip_ids).astype(jnp.float32)
+    qvis = jnp.dot(query_hot, visible.astype(jnp.float32), precision=lax.Precision.HIGHEST).astype(jnp.bfloat16)
+    score_scale = float(np.float32(1.0) / np.sqrt(np.float32(head_size)))
+    local_hot = (clip_group.astype(jnp.int32)[None, :] == clip_ids[0][:, None]).astype(jnp.bfloat16)
+    carry = attend_local(qvis, queries, keys, values, local_hot, score_scale)
     kv_all = lax.all_gather(kv_payload, "x", axis=0)
     key_clips = kv_all[:, 2 * group_tok:2 * group_tok + group_rows].reshape(kv_all.shape[0], group_tok)
     key_hot = (key_clips.astype(jnp.int32)[:, None, :] == clip_ids[0][None, :, None]).astype(jnp.bfloat16)
-    query_hot = (clip_group.astype(jnp.int32)[:, None] == clip_ids).astype(jnp.float32)
-    qvis = jnp.dot(query_hot, visible.astype(jnp.float32), precision=lax.Precision.HIGHEST).astype(jnp.bfloat16)
-    score_scale = float(np.float32(1.0) / np.sqrt(np.float32(head_size)))
-    attended = flash_attention1(qvis, queries, kv_all, key_hot, score_scale, group_tok)
+    own = lax.axis_index("x").reshape(1).astype(jnp.int32)
+    attended = attend_remote(own, qvis, queries, kv_all, key_hot, carry, score_scale, group_tok)
     back = lax.all_to_all(attended.reshape(heads_here, tok, lane), "yc", 0, 0, tiled=True)
     mixed = jnp.einsum(
         "hrd,hdo->ro", back, out_weight, preferred_element_type=jnp.float32

time: 233 us -> 223 us (0.957)
  waiting for transfers between devices: 44.6 us -> 30.7 us
  Pallas kernels: 46.4 us -> 50.4 us
    all_gather x1, waiting for transfers between devices: 44.6 us -> 30.7 us  [per_device(): kv_all = lax.all_gather(kv_payload, 'x', axis=0)]
    pallas_call x1 -> x2, Pallas kernels: 46.4 us -> 50.4 us  [the longest x1 36.9 us: attend_remote(): pl.pallas_call(kernel, grid_spec=grid_spec, out_shape=jax.ShapeDtypeStruc...]
  transfers between devices with their start and end apart: 1 -> 1, of which waited for: 1 -> 1; matrix products, arithmetic and copies ran while one was open for 1% -> 1% of each run, Pallas kernels for 0% -> 6%
where the time goes in v7:
time: 223 us; the launch traced here: 221 us
  blocking collectives  94.2 us (42%)
  Pallas kernels  50.4 us (23%)
  waiting for transfers between devices  30.7 us (14%)
  matrix products  21.9 us (10%)
  between operations  13.5 us (6%)
  other arithmetic  9.32 us (4%)
    all_to_all x1, blocking collectives, per_device(): parts = lax.all_to_all(parts, 'head', 0, 0)  53.5 us
    pallas_call x1, Pallas kernels, attend_remote(): pl.pallas_call(kernel, grid_spec=grid_spec, out_shape=jax.ShapeDtypeStruc...  36.9 us
    all_gather x1, waiting for transfers between devices, per_device(): kv_all = lax.all_gather(kv_payload, 'x', axis=0)  30.7 us
    all_to_all x1, blocking collectives, per_device(): exch = lax.all_to_all(payload, 'yc', 0, 0, tiled=True)  25.9 us
    all_to_all x1, blocking collectives, per_device(): lax.all_to_all(attended.reshape(heads_here, tok, lane), 'yc', 0, 0, tiled...  14.8 us
    pallas_call x1, Pallas kernels, attend_local(): pl.pallas_call(functools.partial(local_kernel, scale=scale), grid=(nsteps...  13.5 us
    dot_general x1, matrix products, per_device(): jnp.einsum('td,dchk->hctk', moduled, qkv_weight, preferred_element_type=j...  10 us
    dot_general x1, matrix products, per_device(): modulation = jnp.dot(level_hot, mod_table, precision=lax.Precision.HIGHEST)  5.59 us
  transfers between devices with their start and end apart: 1, of which 1 were waited for; matrix products, arithmetic and copies ran while one was open for 1% of the time, Pallas kernels for 6%

profile of v7, /device:TPU:6, one launch (start us, length us, event | category | flops | bytes accessed | tf_op | source)
XLA Modules:
  0.0 221.1 jit_solution(3241995311709150454)
XLA Ops:
  6.5 0.0 copy-start
  6.5 0.7 convert_bitcast_fusion.1
  7.3 0.8 select_reduce_fusion
  8.1 5.6 %fusion.2 = bf16[512,4096,1,1]{1,0,3,2:T(8,128)(2,1)S(1)} fusion(f32[16,4096]{1,0:T(8,128)S(1)} %copy-done, bf16[512,4096]{1,0:T(8,128)(2,1)} %param.7, s32[512]{0:T(512)S(1)} %select_reduce_fusion), kind=kOutput, calls=%fused_computation.4 | convolution fusion | flops 411049984 | bytes 8652800 | tf_op jit(solution)/shard_map/dot_general | solution.py:215
  13.7 10.0 %fusion.7 = bf16[4,3,512,128]{3,2,0,1:T(8,128)(2,1)S(1)} fusion(bf16[512,4096,1,1]{1,0,3,2:T(8,128)(2,1)S(1)} %fusion.2, bf16[4096,3,4,128]{3,2,1,0:T(4,128)(2,1)} %param.8), kind=kOutput, calls=%fused_computation.10 | convolution fusion | flops 6443237376 | bytes 18350080 | tf_op jit(solution)/shard_map/td,dchk->hctk/dot_general | solution.py:217
  23.7 0.1 copy.14
  23.9 0.1 pad_maximum_fusion
  24.0 0.0 copy-start.3
  24.0 25.9 %all_to_all.15 = bf16[4,1544,128]{2,1,0:T(8,128)(2,1)S(1)} all-to-all(bf16[4,1544,128]{2,1,0:T(8,128)(2,1)S(1)} %pad_maximum_fusion), channel_id=1, replica_groups=mesh['x'=4,'yc'=4,'head'=8] {'yc'}, dimensions={0} | all-to-all | bytes 3162112 | tf_op jit(solution)/shard_map/all_to_all | solution.py:230
  49.9 1.0 fusion.14
  50.9 1.2 pad_maximum_fusion.1
  52.1 0.0 all-gather.3.cloned.1.call-update
  52.1 1.5 convolution_convert_fusion.qvis_ref
  53.6 0.7 fusion.11.kh_ref
  54.4 0.0 copy-done.1
  54.4 13.5 %shard_map.73 = (f32[2048,128]{1,0:T(8,128)}, f32[2048,128]{1,0:T(8,128)}, f32[2048,128]{1,0:T(8,128)}) custom-call(bf16[2048,64]{1,0:T(8,128)(2,1)} %convolution_convert_fusion.qvis_ref, bf16[2048,128]{1,0:T(8,128)(2,1)} %bitcast.37, bf16[2048,128]{1,0:T(8,128)(2,1)} %bitcast.33, bf16[2048,128]{1,0:T(8,128)(2,1)} %bitcast.35, bf16[64,2048]{1,0:T(8,128)(2,1)} %fusion.11.kh_ref), custom_call_target="tpu_custom_call" | custom-call | flops 2684354560 | bytes 4194304 | tf_op jit(solution)/shard_map/pallas_call | solution.py:134
  67.9 30.7 %all-gather.3.cloned.1.call-done = bf16[16448,128]{1,0:T(8,128)(2,1)} async-done(((bf16[4112,128]{1,0:T(8,128)(2,1)}), bf16[16448,128]{1,0:T(8,128)(2,1)}) %all-gather.3.cloned.1.call-update) | async-done | bytes 4210704 | tf_op jit(solution)/shard_map/all_gather | solution.py:246
  98.6 0.7 convert_bitcast_fusion
  99.3 1.2 fusion.3.kh_ref
  100.5 36.9 %shard_map.74 = bf16[2048,128]{1,0:T(8,128)(2,1)} custom-call(s32[1]{0:T(128)} %bitcast.own_ref, bf16[2048,64]{1,0:T(8,128)(2,1)} %convolution_convert_fusion.qvis_ref, bf16[2048,128]{1,0:T(8,128)(2,1)} %bitcast.38, bf16[4,4112,128]{2,1,0:T(8,128)(2,1)} %bitcast.43, bf16[4,4112,128]{2,1,0:T(8,128)(2,1)} %bitcast.44, bf16[4,64,2048]{2,1,0:T(8,128)(2,1)} %fusion.3.kh_ref, ...), custom_call_target="tpu_custom_call" | custom-call | flops 8053063680 | bytes 7356416 | tf_op jit(solution)/shard_map/pallas_call | solution.py:191
  137.4 14.8 %all_to_all.16 = bf16[4,512,128]{2,1,0:T(8,128)(2,1)S(1)} all-to-all(bf16[4,512,128]{2,1,0:T(8,128)(2,1)} %bitcast.36), channel_id=1, replica_groups=mesh['x'=4,'yc'=4,'head'=8] {'yc'}, dimensions={0} | all-to-all | bytes 1048576 | tf_op jit(solution)/shard_map/all_to_all | solution.py:251
  152.2 4.7 %bitcast_convert_fusion = bf16[512,4096]{1,0:T(8,128)(2,1)S(1)} fusion(bf16[4,512,128]{2,1,0:T(8,128)(2,1)S(1)} %all_to_all.16, bf16[4,128,4096]{2,1,0:T(8,128)(2,1)} %param.9), kind=kOutput, calls=%fused_computation.2 | convolution fusion | flops 2149580800 | bytes 8912896 | tf_op jit(solution)/shard_map/hrd,hdo->ro/dot_general | solution.py:252
  157.0 53.5 %all_to_all.17 = bf16[8,64,4096]{2,1,0:T(8,128)(2,1)} all-to-all(bf16[8,64,4096]{2,1,0:T(8,128)(2,1)S(1)} %bitcast.31), channel_id=1, replica_groups=mesh['x'=4,'yc'=4,'head'=8] {'head'}, dimensions={0} | all-to-all | bytes 8388608 | tf_op jit(solution)/shard_map/all_to_all | solution.py:257
  210.4 3.8 %reduce_sum.22 = bf16[64,4096]{1,0:T(8,128)(2,1)} reduce(bf16[8,64,4096]{2,1,0:T(8,128)(2,1)} %all_to_all.17, bf16[]{:T(256)} %constant.13.clone.1), dimensions={0}, to_apply=%region_1.2 | reduce | flops 1835008 | bytes 4718594 | tf_op jit(solution)/shard_map/reduce_sum | solution.py:258
  (11 shorter events, 0.0 us)
Async XLA Ops:
  6.5 1.5 copy-start
  6.5 92.0 %all-gather.3.cloned.1.call-start = ((), (), s32[]{:S(2)}) async-start(), calls=%async_computation.3 | async-start | bytes 5263360 | tf_op jit(solution)/shard_map/all_gather | solution.py:246
  24.0 28.1 %copy-start.3 = (s32[64,64]{1,0:T(8,128)S(1)}, s32[64,64]{1,0:T(8,128)}, u32[]{:S(2)}) copy-start(s32[64,64]{1,0:T(8,128)} %param.13) | copy-start | bytes 49156
  50.9 3.5 %copy-start.1 = (bf16[4,512,128]{2,1,0:T(8,128)(2,1)}, bf16[4,512,128]{2,1,0:T(8,128)(2,1)S(1)}, u32[]{:S(2)}) copy-start(bf16[4,512,128]{2,1,0:T(8,128)(2,1)S(1)} %get-tuple-element.11) | copy-start | bytes 1572868
  50.9 3.5 %copy-start.2 = (bf16[4,512,128]{2,1,0:T(8,128)(2,1)}, bf16[4,512,128]{2,1,0:T(8,128)(2,1)S(1)}, u32[]{:S(2)}) copy-start(bf16[4,512,128]{2,1,0:T(8,128)(2,1)S(1)} %get-tuple-element.12) | copy-start | bytes 1572868
Sparse Core Ops, SparseCore 0:
  52.2 46.3 all-gather.2

commit v8 on v7

--- a/solution.py
+++ b/solution.py
@@ -156,8 +156,9 @@
     )(qvis, q, keys, values, key_hot)
 
 
-def attend_remote(own, qvis, q, kv_all, key_hot, carry, scale, tok):
+def attend_remote(own, qvis, q, kv_all, key_hot, carry, scale, tok, part, parts):
     nq, hd = q.shape
+    nq = nq // parts
     sources = kv_all.shape[0]
     clip_count = qvis.shape[1]
     bk = math.gcd(tok, 512)
@@ -172,14 +173,14 @@
         num_scalar_prefetch=1,
         grid=(nsteps,),
         in_specs=[
-            pl.BlockSpec((nq, clip_count), lambda j, o: (0, 0)),
-            pl.BlockSpec((nq, hd), lambda j, o: (0, 0)),
+            pl.BlockSpec((nq, clip_count), lambda j, o: (part, 0)),
+            pl.BlockSpec((nq, hd), lambda j, o: (part, 0)),
             pl.BlockSpec((None, bk, hd), lambda j, o: (src(j, o), j % sub, 0)),
             pl.BlockSpec((None, bk, hd), lambda j, o: (src(j, o), sub + j % sub, 0)),
             pl.BlockSpec((None, clip_count, bk), lambda j, o: (src(j, o), 0, j % sub)),
-            pl.BlockSpec((nq, 128), lambda j, o: (0, 0)),
-            pl.BlockSpec((nq, 128), lambda j, o: (0, 0)),
-            pl.BlockSpec((nq, hd), lambda j, o: (0, 0)),
+            pl.BlockSpec((nq, 128), lambda j, o: (part, 0)),
+            pl.BlockSpec((nq, 128), lambda j, o: (part, 0)),
+            pl.BlockSpec((nq, hd), lambda j, o: (part, 0)),
         ],
         out_specs=pl.BlockSpec((nq, hd), lambda j, o: (0, 0)),
         scratch_shapes=[
@@ -208,11 +209,8 @@
     level_count = mod_table.shape[0]
     tok = clip_of.shape[0]
     clip_ids = lax.broadcasted_iota(jnp.int32, (1, clip_count), 1)
-    level_ids = lax.broadcasted_iota(jnp.int32, (1, level_count), 1)
-    tok_hot = clip_of[:, None] == clip_ids
-    level_rows = jnp.sum(jnp.where(tok_hot, clip_level[None, :], 0), axis=1)
-    level_hot = (level_rows[:, None] == level_ids).astype(jnp.float32)
-    modulation = jnp.dot(level_hot, mod_table, precision=lax.Precision.HIGHEST)
+    level_rows = jnp.take(clip_level, clip_of, axis=0)
+    modulation = jnp.take(mod_table, level_rows, axis=0)
     moduled = (activations.astype(jnp.float32) * (1.0 + modulation)).astype(jnp.bfloat16)
     qkv = jnp.einsum(
         "td,dchk->hctk", moduled, qkv_weight, preferred_element_type=jnp.float32
@@ -238,24 +236,39 @@
     kv_payload = jnp.concatenate(
         [keys, values, clip_group.reshape(group_rows, lane), jnp.zeros((kv_pad, lane), jnp.bfloat16)]
     )
-    query_hot = (clip_group.astype(jnp.int32)[:, None] == clip_ids).astype(jnp.float32)
+    blocks = lax.axis_size("head")
+    parts = 2
+    piece = tok // (parts * blocks)
+
+    def split_rows(a):
+        rest = a.shape[1:]
+        a = a.reshape((heads_here, blocks, parts, piece) + rest)
+        return jnp.moveaxis(a, 2, 0).reshape((group_tok,) + rest)
+
+    q_ord = split_rows(queries)
+    clip_q = split_rows(clip_group).astype(jnp.int32)
+    query_hot = (clip_q[:, None] == clip_ids).astype(jnp.float32)
     qvis = jnp.dot(query_hot, visible.astype(jnp.float32), precision=lax.Precision.HIGHEST).astype(jnp.bfloat16)
     score_scale = float(np.float32(1.0) / np.sqrt(np.float32(head_size)))
     local_hot = (clip_group.astype(jnp.int32)[None, :] == clip_ids[0][:, None]).astype(jnp.bfloat16)
-    carry = attend_local(qvis, queries, keys, values, local_hot, score_scale)
+    carry = attend_local(qvis, q_ord, keys, values, local_hot, score_scale)
     kv_all = lax.all_gather(kv_payload, "x", axis=0)
     key_clips = kv_all[:, 2 * group_tok:2 * group_tok + group_rows].reshape(kv_all.shape[0], group_tok)
     key_hot = (key_clips.astype(jnp.int32)[:, None, :] == clip_ids[0][None, :, None]).astype(jnp.bfloat16)
     own = lax.axis_index("x").reshape(1).astype(jnp.int32)
-    attended = attend_remote(own, qvis, queries, kv_all, key_hot, carry, score_scale, group_tok)
-    back = lax.all_to_all(attended.reshape(heads_here, tok, lane), "yc", 0, 0, tiled=True)
-    mixed = jnp.einsum(
-        "hrd,hdo->ro", back, out_weight, preferred_element_type=jnp.float32
-    ).astype(jnp.bfloat16)
-    groups = lax.axis_size("head")
-    parts = mixed.reshape(groups, mixed.shape[0] // groups, mixed.shape[1])
-    parts = lax.all_to_all(parts, "head", 0, 0)
-    return jnp.sum(parts.astype(jnp.float32), axis=0).astype(jnp.bfloat16)
+    outs = []
+    for part in range(parts):
+        attended = attend_remote(own, qvis, q_ord, kv_all, key_hot, carry, score_scale, group_tok, part, parts)
+        back = lax.all_to_all(attended.reshape(heads_here, blocks * piece, lane), "yc", 0, 0, tiled=True)
+        mixed = jnp.einsum(
+            "hrd,hdo->ro", back, out_weight, preferred_element_type=jnp.float32
+        ).astype(jnp.bfloat16)
+        if part == 0:
+            outs.append(lax.psum_scatter(mixed, "head", scatter_dimension=0, tiled=True))
+        else:
+            pieces = lax.all_to_all(mixed.reshape(blocks, piece, mixed.shape[1]), "head", 0, 0)
+            outs.append(jnp.sum(pieces.astype(jnp.float32), axis=0).astype(jnp.bfloat16))
+    return jnp.concatenate(outs, axis=0)
 
 
 def solution(mesh):

time: 223 us -> 275 us (1.23)
  other arithmetic: 9.32 us -> 47.3 us
  local copies, waits for them, and re-layouts: 1.13 us -> 14.2 us
  Pallas kernels: 50.4 us -> 53.7 us
  blocking collectives: 94.2 us -> 91.3 us
    and x0 -> x1, other arithmetic: none -> 40.6 us  [per_device(): modulation = jnp.take(mod_table, level_rows, axis=0)]
    gather x0 -> x5, local copies, waits for them, and re-layouts: none -> 12.9 us  [the longest x4 7.77 us: per_device(): level_rows = jnp.take(clip_level, clip_of, axis=0)]
    dot_general x1 -> x0, matrix products: 5.59 us -> none  [per_device(): modulation = jnp.dot(level_hot, mod_table, precision=lax.Precision.HIGHEST)]
    reduce_sum x2 -> x1, other arithmetic: 4.63 us -> 0.34 us  [per_device(): jnp.sum(pieces.astype(jnp.float32), axis=0).astype(jnp.bfloat16)]
    dot_general x1 -> x2, matrix products: 4.73 us -> 8.35 us  [per_device(): jnp.einsum('hrd,hdo->ro', back, out_weight, preferred_element_type=jnp.fl...]
    dot_general x1, matrix products: 10 us -> 13.5 us  [per_device(): jnp.einsum('td,dchk->hctk', moduled, qkv_weight, preferred_element_type=j...]
    pallas_call x1 -> x2, Pallas kernels: 36.9 us -> 40.1 us  [attend_remote(): pl.pallas_call(kernel, grid_spec=grid_spec, out_shape=jax.ShapeDtypeStruc...]
    all_to_all x2 -> x3, blocking collectives: 68.3 us -> 65.4 us  [the longest x1 39.3 us: per_device(): lax.all_to_all(mixed.reshape(blocks, piece, mixed.shape[1]), 'head', 0, 0)]
  transfers between devices with their start and end apart: 1 -> 2, of which waited for: 1 -> 1; matrix products, arithmetic and copies ran while one was open for 1% -> 3% of each run, Pallas kernels for 6% -> 12%
where the time goes in v8:
time: 275 us; the launch traced here: 273 us
  blocking collectives  91.3 us (33%)
  Pallas kernels  53.7 us (20%)
  other arithmetic  47.3 us (17%)
  waiting for transfers between devices  29.6 us (11%)
  matrix products  23.4 us (9%)
  local copies, waits for them, and re-layouts  14.2 us (5%)
  between operations  13.5 us (5%)
    and x1, other arithmetic, per_device(): modulation = jnp.take(mod_table, level_rows, axis=0)  40.6 us
    pallas_call x2, Pallas kernels, attend_remote(): pl.pallas_call(kernel, grid_spec=grid_spec, out_shape=jax.ShapeDtypeStruc...  40.1 us
    all_to_all x1, blocking collectives, per_device(): lax.all_to_all(mixed.reshape(blocks, piece, mixed.shape[1]), 'head', 0, 0)  39.3 us
    all_gather x1, waiting for transfers between devices, per_device(): kv_all = lax.all_gather(kv_payload, 'x', axis=0)  29.5 us
    all_to_all x2, blocking collectives, per_device(): lax.all_to_all(attended.reshape(heads_here, blocks * piece, lane), 'yc',...  26.1 us
    all_to_all x1, blocking collectives, per_device(): exch = lax.all_to_all(payload, 'yc', 0, 0, tiled=True)  25.9 us
    pallas_call x1, Pallas kernels, attend_local(): pl.pallas_call(functools.partial(local_kernel, scale=scale), grid=(nsteps...  13.6 us
    dot_general x1, matrix products, per_device(): jnp.einsum('td,dchk->hctk', moduled, qkv_weight, preferred_element_type=j...  13.5 us
  transfers between devices with their start and end apart: 2, of which 1 were waited for; matrix products, arithmetic and copies ran while one was open for 3% of the time, Pallas kernels for 12%

profile of v8, /device:TPU:6, one launch (start us, length us, event | category | flops | bytes accessed | tf_op | source)
XLA Modules:
  0.0 273.1 jit_solution(13198944040454536399)
XLA Ops:
  6.5 1.6 fusion.30
  8.1 2.1 fusion.29
  10.2 2.1 fusion.28
  12.3 2.1 fusion.27
  15.0 40.6 %compare_and_fusion = (pred[512]{0:T(512)(128)(4,1)S(1)}, s32[512]{0:T(512)S(1)}) fusion(s32[]{:T(128)} %bitcast.64, s32[]{:T(128)} %bitcast.63, s32[]{:T(128)} %bitcast.62, s32[]{:T(128)} %bitcast.61, s32[]{:T(128)} %bitcast.60, s32[]{:T(128)} %bitcast.59, s32[]{:T(128)} %bitcast.58, s32[]{:T(128)} %bitcast.57, s32[]{:T(128)} %bitcast.56, s32[]{:T(128)} %bitcast.55, ...), kind=kLoop, calls=%fused_computation.32 | loop fusion | flops 71168 | bytes 4864 | tf_op jit(solution)/shard_map/jit(_take)/and | solution.py:213
  55.6 5.1 %gather_fusion = f32[512,4096]{1,0:T(8,128)} fusion(f32[16,4096]{1,0:T(8,128)S(1)} %copy-done, s32[1024]{0:T(1024)S(1)} %pad_clamp_fusion), kind=kCustom, calls=%fused_computation | custom fusion | bytes 16779264 | tf_op jit(solution)/shard_map/jit(_take)/gather | solution.py:213
  60.8 13.5 %fusion.15 = bf16[4,3,512,128]{3,2,0,1:T(8,128)(2,1)S(1)} fusion(bf16[4096,3,4,128]{3,2,1,0:T(4,128)(2,1)} %param.8, f32[512,4096]{1,0:T(8,128)} %gather_fusion, bf16[512,4096]{1,0:T(8,128)(2,1)} %param.7, pred[512]{0:T(512)(128)(4,1)S(1)} %get-tuple-element.11), kind=kOutput, calls=%fused_computation.17 | convolution fusion | flops 6453723136 | bytes 26739200 | tf_op jit(solution)/shard_map/td,dchk->hctk/dot_general | solution.py:215
  74.5 25.9 %all_to_all.20 = bf16[4,1544,128]{2,1,0:T(8,128)(2,1)S(1)} all-to-all(bf16[4,1544,128]{2,1,0:T(8,128)(2,1)S(1)} %pad_maximum_fusion), channel_id=1, replica_groups=mesh['x'=4,'yc'=4,'head'=8] {'yc'}, dimensions={0} | all-to-all | bytes 3162112 | tf_op jit(solution)/shard_map/all_to_all | solution.py:228
  100.6 1.1 pad_maximum_fusion.1
  102.0 0.9 copy.14
  102.8 1.5 convolution_convert_fusion.qvis_ref
  104.3 0.8 fusion.21.kh_ref
  105.1 13.6 %shard_map.73 = (f32[2048,128]{1,0:T(8,128)}, f32[2048,128]{1,0:T(8,128)}, f32[2048,128]{1,0:T(8,128)}) custom-call(bf16[2048,64]{1,0:T(8,128)(2,1)} %convolution_convert_fusion.qvis_ref, bf16[2048,128]{1,0:T(8,128)(2,1)} %bitcast.120, bf16[2048,128]{1,0:T(8,128)(2,1)} %bitcast.117, bf16[2048,128]{1,0:T(8,128)(2,1)} %bitcast.119, bf16[64,2048]{1,0:T(8,128)(2,1)} %fusion.21.kh_ref), custom_call_target="tpu_custom_call" | custom-call | flops 2684354560 | bytes 4194304 | tf_op jit(solution)/shard_map/pallas_call | solution.py:134
  118.7 29.5 %all-gather.3.cloned.1.call-done = bf16[16448,128]{1,0:T(8,128)(2,1)} async-done(((bf16[4112,128]{1,0:T(8,128)(2,1)}), bf16[16448,128]{1,0:T(8,128)(2,1)}) %all-gather.3.cloned.1.call-update) | async-done | bytes 4210704 | tf_op jit(solution)/shard_map/all_gather | solution.py:255
  148.2 0.7 convert_bitcast_fusion
  149.0 1.2 fusion.9.kh_ref
  150.2 20.0 %shard_map.74 = bf16[1024,128]{1,0:T(8,128)(2,1)} custom-call(s32[1]{0:T(128)} %bitcast.own_ref, bf16[2048,64]{1,0:T(8,128)(2,1)} %convolution_convert_fusion.qvis_ref, bf16[2048,128]{1,0:T(8,128)(2,1)} %bitcast.121, bf16[4,4112,128]{2,1,0:T(8,128)(2,1)} %bitcast.130, bf16[4,4112,128]{2,1,0:T(8,128)(2,1)} %bitcast.131, bf16[4,64,2048]{2,1,0:T(8,128)(2,1)} %fusion.9.kh_ref, ...), custom_call_target="tpu_custom_call" | custom-call | flops 4026531840 | bytes 5783552 | tf_op jit(solution)/shard_map/pallas_call | solution.py:192
  170.1 12.0 %all_to_all.21 = bf16[4,256,128]{2,1,0:T(8,128)(2,1)S(1)} all-to-all(bf16[4,256,128]{2,1,0:T(8,128)(2,1)} %bitcast.124), channel_id=1, replica_groups=mesh['x'=4,'yc'=4,'head'=8] {'yc'}, dimensions={0} | all-to-all | bytes 524288 | tf_op jit(solution)/shard_map/all_to_all | solution.py:262
  182.1 4.8 %fusion.2 = bf16[256,4096]{1,0:T(8,128)(2,1)} fusion(bf16[4,256,128]{2,1,0:T(8,128)(2,1)S(1)} %all_to_all.21, bf16[4,128,4096]{2,1,0:T(8,128)(2,1)} %param.9), kind=kOutput, calls=%fused_computation.6 | convolution fusion | flops 1074790400 | bytes 6553600 | tf_op jit(solution)/shard_map/hrd,hdo->ro/dot_general | solution.py:263
  187.0 20.1 %shard_map.75 = bf16[1024,128]{1,0:T(8,128)(2,1)} custom-call(s32[1]{0:T(128)} %bitcast.own_ref, bf16[2048,64]{1,0:T(8,128)(2,1)} %convolution_convert_fusion.qvis_ref, bf16[2048,128]{1,0:T(8,128)(2,1)} %bitcast.122, bf16[4,4112,128]{2,1,0:T(8,128)(2,1)} %bitcast.132, bf16[4,4112,128]{2,1,0:T(8,128)(2,1)} %bitcast.133, bf16[4,64,2048]{2,1,0:T(8,128)(2,1)} %fusion.9.kh_ref, ...), custom_call_target="tpu_custom_call" | custom-call | flops 4026531840 | bytes 5783552 | tf_op jit(solution)/shard_map/pallas_call | solution.py:192
  207.1 14.1 %all_to_all.22 = bf16[4,256,128]{2,1,0:T(8,128)(2,1)S(1)} all-to-all(bf16[4,256,128]{2,1,0:T(8,128)(2,1)} %bitcast.123), channel_id=1, replica_groups=mesh['x'=4,'yc'=4,'head'=8] {'yc'}, dimensions={0} | all-to-all | bytes 524288 | tf_op jit(solution)/shard_map/all_to_all | solution.py:262
  221.2 3.5 %fusion.3 = bf16[256,4096]{1,0:T(8,128)(2,1)S(1)} fusion(bf16[4,256,128]{2,1,0:T(8,128)(2,1)S(1)} %all_to_all.22, bf16[4,128,4096]{2,1,0:T(8,128)(2,1)} %param.9), kind=kOutput, calls=%fused_computation.7 | convolution fusion | flops 1074790400 | bytes 6553600 | tf_op jit(solution)/shard_map/hrd,hdo->ro/dot_general | solution.py:263
  224.7 39.3 %all_to_all.23 = bf16[8,32,4096]{2,1,0:T(8,128)(2,1)S(1)} all-to-all(bf16[8,32,4096]{2,1,0:T(8,128)(2,1)S(1)} %bitcast.114), channel_id=1, replica_groups=mesh['x'=4,'yc'=4,'head'=8] {'head'}, dimensions={0} | all-to-all | bytes 4194304 | tf_op jit(solution)/shard_map/all_to_all | solution.py:269
  264.4 1.8 pad_maximum_fusion.2
  (26 shorter events, 1.7 us)
Async XLA Ops:
  6.5 49.1 %copy-start = (f32[16,4096]{1,0:T(8,128)S(1)}, f32[16,4096]{1,0:T(8,128)}, u32[]{:S(2)}) copy-start(f32[16,4096]{1,0:T(8,128)} %param.10) | copy-start | bytes 786436
  6.5 141.7 %all-gather.3.cloned.1.call-start = ((), (), s32[]{:S(2)}) async-start(), calls=%async_computation.6 | async-start | bytes 5263360 | tf_op jit(solution)/shard_map/all_gather | solution.py:255
  100.4 2.4 copy-start.3
  100.6 4.6 %copy-start.1 = (bf16[4,512,128]{2,1,0:T(8,128)(2,1)}, bf16[4,512,128]{2,1,0:T(8,128)(2,1)S(1)}, u32[]{:S(2)}) copy-start(bf16[4,512,128]{2,1,0:T(8,128)(2,1)S(1)} %get-tuple-element.13) | copy-start | bytes 1572868
  100.6 4.5 %copy-start.2 = (bf16[4,512,128]{2,1,0:T(8,128)(2,1)}, bf16[4,512,128]{2,1,0:T(8,128)(2,1)S(1)}, u32[]{:S(2)}) copy-start(bf16[4,512,128]{2,1,0:T(8,128)(2,1)S(1)} %get-tuple-element.14) | copy-start | bytes 1572868
  101.7 162.7 %reduce-scatter.2.cloned.1.call-start = ((), (), s32[]{:S(2)}) async-start(), calls=%async_computation.5 | async-start | bytes 2359296 | tf_op jit(solution)/shard_map/reduce_scatter | solution.py:267
Sparse Core Ops, SparseCore 0:
  101.8 46.3 all-gather.2
  187.1 62.3 reduce-scatter.1
